TPU v7x, 256 devices: a whole 4x4x8 slice. The times are simulated.
256 devices in a mesh: rad: 8 (over z_hi, core), azi: 32 (over y, x, z_lo).
Axes of the slice: x: 4, y: 4, z: 8 (z_hi: 4, z_lo: 2; z = z_hi * 2 + z_lo), core: 2. Of those that a mesh axis runs over, the one named last changes fastest.
Arguments:
- gas_state: float32 [4, 16, 512, 1024], P(None, None, 'azi', 'rad'), may hold values from -6 to 6
- sound_sq: float32 [16, 512, 1024], P(None, 'azi', 'rad'), may hold values from 0.5 to 2
- offsets: int32 [1024], P('rad'), may hold values from 0 to 511
Outputs:
- final_state: float32 [4, 16, 512, 1024], P(None, None, 'azi', 'rad')
All inputs are finite; a program needn't handle non-finite values.
Results may differ from a plain program's by a relative error of at most 0.00002.
Values sent between devices are 32-bit elements; how exact they have to be, the bound alone decides.
No kernel may reach another device: no remote copies, remote signals or barrier semaphores. Data moves between devices by JAX's collectives and lax.ppermute only.
A program may use at most 64 MiB of HBM per device.

v0:
```python
import jax
import jax.numpy as jnp
from jax import lax
from jax.sharding import PartitionSpec as P
from jax.experimental import pallas as pl
from jax.experimental.pallas import tpu as pltpu

ORDER = 4
STEPS = 2


TIME_STEP = 0.5
ANGULAR_RATE = 1.0
SHEAR_RATE = 1.5


def ring(axis, by):
    count = lax.axis_size(axis)
    return [(i, (i + by) % count) for i in range(count)]


def window(values, start, length, which_dim):
    return lax.slice_in_dim(values, start, start + length, axis=which_dim)


def diff_along(values, which_dim):
    length = values.shape[which_dim] - 4
    return (
        8.0 * (window(values, 3, length, which_dim) - window(values, 1, length, which_dim))
        - (window(values, 4, length, which_dim) - window(values, 0, length, which_dim))
    ) / 12.0


def diff_vertical(values):
    return (
        8.0 * (jnp.roll(values, -1, 0) - jnp.roll(values, 1, 0))
        - (jnp.roll(values, -2, 0) - jnp.roll(values, 2, 0))
    ) / 12.0


def extended(cells, depth):
    count = cells.shape[2]
    cells = jnp.concatenate(
        [
            lax.ppermute(cells[:, :, count - depth:, :], "azi", ring("azi", 1)),
            cells,
            lax.ppermute(cells[:, :, :depth, :], "azi", ring("azi", -1)),
        ],
        axis=2,
    )
    rows = cells.shape[3]
    low = jnp.swapaxes(cells[..., rows - depth:], 2, 3)
    high = jnp.swapaxes(cells[..., :depth], 2, 3)
    low = jnp.swapaxes(lax.ppermute(low, "rad", ring("rad", 1)), 2, 3)
    high = jnp.swapaxes(lax.ppermute(high, "rad", ring("rad", -1)), 2, 3)
    return jnp.concatenate([low, cells, high], axis=3)


def inside_rows(start, extent, depth, row_count):
    global_row = (
        lax.axis_index("rad") * row_count - depth + start + jnp.arange(extent, dtype=jnp.int32)
    )
    return (global_row >= 0) & (global_row < row_count * lax.axis_size("rad"))


def operator_core(pressure, radial_flow, azimuth_flow, vertical_flow):
    density_rate = -(
        diff_along(radial_flow[:, 2:-2, :], 2)
        + diff_along(azimuth_flow[:, :, 2:-2], 1)
        + diff_vertical(inner_part(vertical_flow))
    )
    radial_rate = -diff_along(pressure[:, 2:-2, :], 2) + 2.0 * ANGULAR_RATE * inner_part(
        azimuth_flow
    )
    azimuth_rate = -diff_along(pressure[:, :, 2:-2], 1) - (
        2.0 - SHEAR_RATE
    ) * ANGULAR_RATE * inner_part(radial_flow)
    vertical_rate = -diff_vertical(inner_part(pressure))
    return jnp.stack([density_rate, radial_rate, azimuth_rate, vertical_rate])


def inner_part(values):
    return values[:, 2:-2, 2:-2]


def lane_diff(values):
    size = values.shape[1]
    return (
        8.0 * (pltpu.roll(values, size - 1, 1) - pltpu.roll(values, 1, 1))
        - (pltpu.roll(values, size - 2, 1) - pltpu.roll(values, 2, 1))
    ) / 12.0


def sublane_diff(values):
    size = values.shape[0]
    return (
        8.0 * (pltpu.roll(values, size - 1, 0) - pltpu.roll(values, 1, 0))
        - (pltpu.roll(values, size - 2, 0) - pltpu.roll(values, 2, 0))
    ) / 12.0


def taylor_kernel(keep_ref, sound_ref, state_ref, running_ref, even_ref, odd_ref):
    keep = keep_ref[...] != 0.0
    levels = state_ref.shape[1]

    def start(level, carry):
        for field in range(4):
            values = state_ref[field, level]
            running_ref[field, level] = values
            even_ref[field, level] = jnp.where(keep, values, 0.0)
        return carry

    lax.fori_loop(0, levels, start, 0)
    for degree in range(1, ORDER + 1):
        source, target = (even_ref, odd_ref) if degree % 2 else (odd_ref, even_ref)

        def order(level, carry, source=source, target=target, scale=TIME_STEP / degree):
            near = [lax.rem(level + step + levels, levels) for step in (1, -1, 2, -2)]

            def vertical(value_at):
                up1, down1, up2, down2 = (value_at(at) for at in near)
                return (8.0 * (up1 - down1) - (up2 - down2)) / 12.0

            radial_flow = source[1, level]
            azimuth_flow = source[2, level]
            pressure = sound_ref[level] * source[0, level]
            density_rate = -(
                lane_diff(radial_flow)
                + sublane_diff(azimuth_flow)
                + vertical(lambda at: source[3, at])
            )
            radial_rate = -lane_diff(pressure) + 2.0 * ANGULAR_RATE * azimuth_flow
            azimuth_rate = -sublane_diff(pressure) - (2.0 - SHEAR_RATE) * ANGULAR_RATE * radial_flow
            vertical_rate = -vertical(lambda at: sound_ref[at] * source[0, at])
            rates = (density_rate, radial_rate, azimuth_rate, vertical_rate)
            for field, rate in enumerate(rates):
                series = jnp.where(keep, scale * rate, 0.0)
                target[field, level] = series
                running_ref[field, level] = running_ref[field, level] + series
            return carry

        lax.fori_loop(0, levels, order, 0)


def taylor(wide_state, wide_sound, depth, cells, row_count):
    lanes = 128 * -(-wide_state.shape[3] // 128)
    extra = lanes - wide_state.shape[3]
    wide_state = jnp.pad(wide_state, ((0, 0), (0, 0), (0, 0), (0, extra)))
    wide_sound = jnp.pad(wide_sound, ((0, 0), (0, 0), (0, extra)))
    keep = inside_rows(0, lanes, depth, row_count).astype(jnp.float32)[None, :]
    whole = pl.BlockSpec(memory_space=pltpu.VMEM)
    size = wide_state.size
    running = pl.pallas_call(
        taylor_kernel,
        out_shape=jax.ShapeDtypeStruct(wide_state.shape, jnp.float32),
        in_specs=[whole, whole, whole],
        out_specs=whole,
        scratch_shapes=[pltpu.VMEM(wide_state.shape, jnp.float32)] * 2,
        compiler_params=pltpu.CompilerParams(vmem_limit_bytes=48 * 1024 * 1024),
        cost_estimate=pl.CostEstimate(
            flops=60 * ORDER * size, transcendentals=0, bytes_accessed=4 * (2 * size + size // 4)
        ),
    )(keep, wide_sound, wide_state)
    return running[:, :, depth:depth + cells, depth:depth + row_count]


def roll_cells(blocks, shift):
    cells = blocks.shape[2]
    whole, part = divmod(shift, cells)
    if whole:
        blocks = jnp.roll(blocks, whole, axis=0)
    if part:
        carried = jnp.roll(blocks, 1, axis=0)
        blocks = jnp.concatenate(
            [carried[:, :, cells - part:], blocks[:, :, :cells - part]], axis=2
        )
    return blocks


def remap(state, offsets):
    fields, levels, cells, rows = state.shape
    peers = lax.axis_size("azi")
    planes = state.reshape(peers, fields * levels // peers, cells, rows)
    blocks = lax.all_to_all(planes, "azi", 0, 0, tiled=True)
    total = peers * cells
    for bit_pos in range((total - 1).bit_length()):
        chosen = (offsets >> bit_pos) & 1 == 1
        blocks = jnp.where(chosen, roll_cells(blocks, 1 << bit_pos), blocks)
    planes = lax.all_to_all(blocks, "azi", 0, 0, tiled=True)
    return planes.reshape(fields, levels, cells, rows)


def per_device(gas_state, sound_sq, offsets):
    depth = 2 * ORDER
    cells, row_count = gas_state.shape[2], gas_state.shape[3]
    wide = extended(jnp.concatenate([gas_state, sound_sq[None]]), depth)
    wide_state, wide_sound = wide[:4], wide[4]
    for timestep in range(STEPS):
        if timestep:
            wide_state = extended(state, depth)
        running = taylor(wide_state, wide_sound, depth, cells, row_count)
        state = remap(running, offsets)
    return state


def solution(mesh):
    in_specs = (P(None, None, "azi", "rad"), P(None, "azi", "rad"), P("rad"))
    out_specs = P(None, None, "azi", "rad")
    return jax.shard_map(
        per_device, mesh=mesh, in_specs=in_specs, out_specs=out_specs, check_vma=False
    )
```

profile of v0, /device:TPU:64, one launch (start us, length us, event | category | flops | bytes accessed | tf_op | source)
XLA Modules:
  0.0 161.1 jit_solution(9167879257372982962)
XLA Ops:
  0.0 1.1 fusion.32
  1.1 2.0 %collective-permute-start = (f32[5,16,8,128]{3,2,1,0:T(8,128)S(1)}, f32[5,16,8,128]{3,2,1,0:T(8,128)S(1)}, u32[]{:S(2)}, u32[]{:S(2)}) collective-permute-start(f32[5,16,8,128]{3,2,1,0:T(8,128)S(1)} %get-tuple-element.9), channel_id=1, source_target_pairs={{0,1},{1,2},{2,3},{3,4},{4,5},{5,6},{6,7},{7,8},{8,9},{9,10},{10,1... | collective-permute-start | bytes 983048 | tf_op jit(solution)/shard_map/ppermute | solution.py:45
  3.1 4.7 %collective-permute-start.1 = (f32[5,16,8,128]{3,2,1,0:T(8,128)S(1)}, f32[5,16,8,128]{3,2,1,0:T(8,128)S(1)}, u32[]{:S(2)}, u32[]{:S(2)}) collective-permute-start(f32[5,16,8,128]{3,2,1,0:T(8,128)S(1)} %get-tuple-element.10), channel_id=1, source_target_pairs={{0,31},{1,0},{2,1},{3,2},{4,3},{5,4},{6,5},{7,6},{8,7},{9,8},{10,9... | collective-permute-start | bytes 983048 | tf_op jit(solution)/shard_map/ppermute | solution.py:47
  7.8 8.5 %collective-permute-done = f32[5,16,8,128]{3,2,1,0:T(8,128)S(1)} collective-permute-done((f32[5,16,8,128]{3,2,1,0:T(8,128)S(1)}, f32[5,16,8,128]{3,2,1,0:T(8,128)S(1)}, u32[]{:S(2)}, u32[]{:S(2)}) %collective-permute-start) | collective-permute-done | bytes 327712 | tf_op jit(solution)/shard_map/ppermute | solution.py:45
  16.3 2.3 %collective-permute-done.1 = f32[5,16,8,128]{3,2,1,0:T(8,128)S(1)} collective-permute-done((f32[5,16,8,128]{3,2,1,0:T(8,128)S(1)}, f32[5,16,8,128]{3,2,1,0:T(8,128)S(1)}, u32[]{:S(2)}, u32[]{:S(2)}) %collective-permute-start.1) | collective-permute-done | bytes 327712 | tf_op jit(solution)/shard_map/ppermute | solution.py:47
  18.6 1.4 pad_maximum_fusion
  20.4 1.1 copy.4
  21.9 2.7 %collective-permute-start.3 = (f32[5,16,8,32]{3,2,1,0:T(8,128)S(1)}, f32[5,16,8,32]{3,2,1,0:T(8,128)}, u32[]{:S(2)}, u32[]{:S(2)}) collective-permute-start(f32[5,16,8,32]{3,2,1,0:T(8,128)S(1)} %copy.6), channel_id=1, source_target_pairs={{0,224},{32,0},{64,32},{96,64},{128,96},{160,128},{192,160},{224,1... | collective-permute-start | bytes 245768 | tf_op jit(solution)/shard_map/ppermute | solution.py:55
  24.6 5.2 %collective-permute-done.2 = f32[5,16,8,32]{3,2,1,0:T(8,128)S(1)} collective-permute-done((f32[5,16,8,32]{3,2,1,0:T(8,128)}, f32[5,16,8,32]{3,2,1,0:T(8,128)S(1)}, u32[]{:S(2)}, u32[]{:S(2)}) %collective-permute-start.2) | collective-permute-done | bytes 81952 | tf_op jit(solution)/shard_map/ppermute | solution.py:54
  30.2 2.5 %collective-permute-done.3 = f32[5,16,8,32]{3,2,1,0:T(8,128)} collective-permute-done((f32[5,16,8,32]{3,2,1,0:T(8,128)S(1)}, f32[5,16,8,32]{3,2,1,0:T(8,128)}, u32[]{:S(2)}, u32[]{:S(2)}) %collective-permute-start.3) | collective-permute-done | bytes 81952 | tf_op jit(solution)/shard_map/ppermute | solution.py:55
  32.8 1.4 copy.7
  34.2 1.3 maximum_bitcast_fusion
  35.6 0.9 fusion.10.state_ref
  36.5 9.7 %shard_map.37 = f32[4,16,32,256]{3,2,1,0:T(8,128)S(1)} custom-call(f32[1,256]{1,0:T(1,128)S(1)} %and_convert_fusion.keep_ref, f32[16,32,256]{2,1,0:T(8,128)S(1)} %pad.12.sound_ref, f32[4,16,32,256]{3,2,1,0:T(8,128)S(1)} %fusion.10.state_ref), custom_call_target="tpu_custom_call" | custom-call | flops 125829120 | bytes 4718592 | tf_op jit(solution)/shard_map/pallas_call | solution.py:153
  46.3 1.0 slice.270
  47.2 8.4 %all-to-all-start = ((f32[32,2,16,128]{3,2,1,0:T(8,128)}), f32[32,2,16,128]{3,2,1,0:T(8,128)S(1)}, u32[]{:S(2)}, u32[]{:S(2)}) async-start(f32[32,2,16,128]{3,2,1,0:T(8,128)} %bitcast.6), calls=%async_computation | async-start | bytes 1048576 | tf_op jit(solution)/shard_map/all_to_all | solution.py:184
  55.6 11.2 %all-to-all-done = f32[32,2,16,128]{3,2,1,0:T(8,128)S(1)} async-done(((f32[32,2,16,128]{3,2,1,0:T(8,128)}), f32[32,2,16,128]{3,2,1,0:T(8,128)S(1)}, u32[]{:S(2)}, u32[]{:S(2)}) %all-to-all-start) | async-done | bytes 524320 | tf_op jit(solution)/shard_map/all_to_all | solution.py:184
  68.2 15.4 %all_to_all.20 = f32[32,2,16,128]{3,2,1,0:T(8,128)S(1)} all-to-all(f32[32,2,16,128]{3,2,1,0:T(8,128)S(1)} %maximum_select_fusion.4), channel_id=1, replica_groups=mesh['rad'=8,'azi'=32] {'azi'}, dimensions={0} | all-to-all | bytes 1048576 | tf_op jit(solution)/shard_map/all_to_all | solution.py:189
  83.8 6.2 %collective-permute-start.5 = (f32[4,16,8,128]{3,2,1,0:T(8,128)S(1)}, f32[4,16,8,128]{3,2,1,0:T(8,128)S(1)}, u32[]{:S(2)}, u32[]{:S(2)}) collective-permute-start(f32[4,16,8,128]{3,2,1,0:T(8,128)S(1)} %get-tuple-element.14), channel_id=1, source_target_pairs={{0,31},{1,0},{2,1},{3,2},{4,3},{5,4},{6,5},{7,6},{8,7},{9,8},{10,9... | collective-permute-start | bytes 786440 | tf_op jit(solution)/shard_map/ppermute | solution.py:47
  89.9 6.8 %collective-permute-done.4 = f32[4,16,8,128]{3,2,1,0:T(8,128)S(1)} collective-permute-done((f32[4,16,8,128]{3,2,1,0:T(8,128)S(1)}, f32[4,16,8,128]{3,2,1,0:T(8,128)S(1)}, u32[]{:S(2)}, u32[]{:S(2)}) %collective-permute-start.4) | collective-permute-done | bytes 262176 | tf_op jit(solution)/shard_map/ppermute | solution.py:45
  96.7 1.0 collective-permute-done.5
  97.8 0.7 copy-done.5
  98.9 1.0 copy.10
  100.3 0.7 collective-permute-start.6
  101.0 5.1 %collective-permute-done.7 = f32[4,16,8,32]{3,2,1,0:T(8,128)S(1)} collective-permute-done((f32[4,16,8,32]{3,2,1,0:T(8,128)}, f32[4,16,8,32]{3,2,1,0:T(8,128)S(1)}, u32[]{:S(2)}, u32[]{:S(2)}) %collective-permute-start.7) | collective-permute-done | bytes 65568 | tf_op jit(solution)/shard_map/ppermute | solution.py:55
  106.5 3.5 %collective-permute-done.6 = f32[4,16,8,32]{3,2,1,0:T(8,128)} collective-permute-done((f32[4,16,8,32]{3,2,1,0:T(8,128)S(1)}, f32[4,16,8,32]{3,2,1,0:T(8,128)}, u32[]{:S(2)}, u32[]{:S(2)}) %collective-permute-start.6) | collective-permute-done | bytes 65568 | tf_op jit(solution)/shard_map/ppermute | solution.py:54
  110.0 1.3 copy.9
  111.3 1.8 %select_maximum_fusion.state_ref = f32[4,16,32,256]{3,2,1,0:T(8,128)S(1)} fusion(f32[4,16,32,8]{3,2,1,0:T(8,128)S(1)} %bitcast.38, f32[4,16,32,8]{3,2,1,0:T(8,128)S(1)} %bitcast.39, f32[4,16,8,128]{3,2,1,0:T(8,128)} %copy-done.5, f32[4,16,16,128]{3,2,1,0:T(8,128)S(1)} %bitcast.37, f32[4,16,8,128]{3,2,1,0:T(8,128)S(1)} %collective-permute-done.4), kind=kLoop, calls=%fused_computation | loop fusion | flops 5242880 | bytes 3276800 | tf_op jit(solution)/shard_map/concatenate | solution.py:56
  113.2 9.7 %shard_map.38 = f32[4,16,32,256]{3,2,1,0:T(8,128)S(1)} custom-call(f32[1,256]{1,0:T(1,128)S(1)} %and_convert_fusion.keep_ref, f32[16,32,256]{2,1,0:T(8,128)S(1)} %pad.12.sound_ref, f32[4,16,32,256]{3,2,1,0:T(8,128)S(1)} %select_maximum_fusion.state_ref), custom_call_target="tpu_custom_call" | custom-call | flops 125829120 | bytes 4718592 | tf_op jit(solution)/shard_map/pallas_call | solution.py:153
  123.1 20.5 %all_to_all.21 = f32[32,2,16,128]{3,2,1,0:T(8,128)S(1)} all-to-all(f32[32,2,16,128]{3,2,1,0:T(8,128)S(1)} %bitcast.44), channel_id=1, replica_groups=mesh['rad'=8,'azi'=32] {'azi'}, dimensions={0} | all-to-all | bytes 1048576 | tf_op jit(solution)/shard_map/all_to_all | solution.py:184
  145.0 15.3 %all_to_all.22 = f32[32,2,16,128]{3,2,1,0:T(8,128)S(1)} all-to-all(f32[32,2,16,128]{3,2,1,0:T(8,128)S(1)} %maximum_select_fusion.9), channel_id=1, replica_groups=mesh['rad'=8,'azi'=32] {'azi'}, dimensions={0} | all-to-all | bytes 1048576 | tf_op jit(solution)/shard_map/all_to_all | solution.py:189
  160.3 0.8 copy.13
  (82 shorter events, 5.3 us)
Async XLA Ops:
  1.1 15.2 %collective-permute-start = (f32[5,16,8,128]{3,2,1,0:T(8,128)S(1)}, f32[5,16,8,128]{3,2,1,0:T(8,128)S(1)}, u32[]{:S(2)}, u32[]{:S(2)}) collective-permute-start(f32[5,16,8,128]{3,2,1,0:T(8,128)S(1)} %get-tuple-element.9), channel_id=1, source_target_pairs={{0,1},{1,2},{2,3},{3,4},{4,5},{5,6},{6,7},{7,8},{8,9},{9,10},{10,1... | collective-permute-start | bytes 983048 | tf_op jit(solution)/shard_map/ppermute | solution.py:45
  3.1 15.5 %collective-permute-start.1 = (f32[5,16,8,128]{3,2,1,0:T(8,128)S(1)}, f32[5,16,8,128]{3,2,1,0:T(8,128)S(1)}, u32[]{:S(2)}, u32[]{:S(2)}) collective-permute-start(f32[5,16,8,128]{3,2,1,0:T(8,128)S(1)} %get-tuple-element.10), channel_id=1, source_target_pairs={{0,31},{1,0},{2,1},{3,2},{4,3},{5,4},{6,5},{7,6},{8,7},{9,8},{10,9... | collective-permute-start | bytes 983048 | tf_op jit(solution)/shard_map/ppermute | solution.py:47
  18.6 1.8 %copy-start.2 = (f32[5,16,8,128]{3,2,1,0:T(8,128)}, f32[5,16,8,128]{3,2,1,0:T(8,128)S(1)}, u32[]{:S(2)}) copy-start(f32[5,16,8,128]{3,2,1,0:T(8,128)S(1)} %collective-permute-done.1) | copy-start | bytes 983044
  21.5 8.3 %collective-permute-start.2 = (f32[5,16,8,32]{3,2,1,0:T(8,128)}, f32[5,16,8,32]{3,2,1,0:T(8,128)S(1)}, u32[]{:S(2)}, u32[]{:S(2)}) collective-permute-start(f32[5,16,8,32]{3,2,1,0:T(8,128)} %copy.4), channel_id=1, source_target_pairs={{0,32},{32,64},{64,96},{96,128},{128,160},{160,192},{192,224},{224... | collective-permute-start | bytes 245768 | tf_op jit(solution)/shard_map/ppermute | solution.py:54
  21.5 12.6 %copy-start = (f32[4,16,16,128]{3,2,1,0:T(8,128)S(1)}, f32[4,16,16,128]{3,2,1,0:T(8,128)}, u32[]{:S(2)}) copy-start(f32[4,16,16,128]{3,2,1,0:T(8,128)} %param.3) | copy-start | bytes 1572868
  21.9 10.8 %collective-permute-start.3 = (f32[5,16,8,32]{3,2,1,0:T(8,128)S(1)}, f32[5,16,8,32]{3,2,1,0:T(8,128)}, u32[]{:S(2)}, u32[]{:S(2)}) collective-permute-start(f32[5,16,8,32]{3,2,1,0:T(8,128)S(1)} %copy.6), channel_id=1, source_target_pairs={{0,224},{32,0},{64,32},{96,64},{128,96},{160,128},{192,160},{224,1... | collective-permute-start | bytes 245768 | tf_op jit(solution)/shard_map/ppermute | solution.py:55
  34.2 1.4 copy-start.1
  34.2 1.4 copy-start.3
  34.2 1.4 copy-start.4
  46.2 9.4 %copy-start.6 = (s32[128]{0:T(128)S(1)}, s32[128]{0:T(128)}, u32[]{:S(2)}) copy-start(s32[128]{0:T(128)} %param.5) | copy-start | bytes 1540
  47.2 19.6 %all-to-all-start = ((f32[32,2,16,128]{3,2,1,0:T(8,128)}), f32[32,2,16,128]{3,2,1,0:T(8,128)S(1)}, u32[]{:S(2)}, u32[]{:S(2)}) async-start(f32[32,2,16,128]{3,2,1,0:T(8,128)} %bitcast.6), calls=%async_computation | async-start | bytes 1048576 | tf_op jit(solution)/shard_map/all_to_all | solution.py:184
  83.6 13.1 %collective-permute-start.4 = (f32[4,16,8,128]{3,2,1,0:T(8,128)S(1)}, f32[4,16,8,128]{3,2,1,0:T(8,128)S(1)}, u32[]{:S(2)}, u32[]{:S(2)}) collective-permute-start(f32[4,16,8,128]{3,2,1,0:T(8,128)S(1)} %get-tuple-element.13), channel_id=1, source_target_pairs={{0,1},{1,2},{2,3},{3,4},{4,5},{5,6},{6,7},{7,8},{8,9},{9,10},{10,1... | collective-permute-start | bytes 786440 | tf_op jit(solution)/shard_map/ppermute | solution.py:45
  83.8 14.0 %collective-permute-start.5 = (f32[4,16,8,128]{3,2,1,0:T(8,128)S(1)}, f32[4,16,8,128]{3,2,1,0:T(8,128)S(1)}, u32[]{:S(2)}, u32[]{:S(2)}) collective-permute-start(f32[4,16,8,128]{3,2,1,0:T(8,128)S(1)} %get-tuple-element.14), channel_id=1, source_target_pairs={{0,31},{1,0},{2,1},{3,2},{4,3},{5,4},{6,5},{7,6},{8,7},{9,8},{10,9... | collective-permute-start | bytes 786440 | tf_op jit(solution)/shard_map/ppermute | solution.py:47
  97.8 0.7 copy-start.5
  100.0 6.2 %collective-permute-start.7 = (f32[4,16,8,32]{3,2,1,0:T(8,128)}, f32[4,16,8,32]{3,2,1,0:T(8,128)S(1)}, u32[]{:S(2)}, u32[]{:S(2)}) collective-permute-start(f32[4,16,8,32]{3,2,1,0:T(8,128)} %copy.10), channel_id=1, source_target_pairs={{0,224},{32,0},{64,32},{96,64},{128,96},{160,128},{192,160},{224,1... | collective-permute-start | bytes 196616 | tf_op jit(solution)/shard_map/ppermute | solution.py:55
  100.3 9.7 %collective-permute-start.6 = (f32[4,16,8,32]{3,2,1,0:T(8,128)S(1)}, f32[4,16,8,32]{3,2,1,0:T(8,128)}, u32[]{:S(2)}, u32[]{:S(2)}) collective-permute-start(f32[4,16,8,32]{3,2,1,0:T(8,128)S(1)} %copy.8), channel_id=1, source_target_pairs={{0,32},{32,64},{64,96},{96,128},{128,160},{160,192},{192,224},{224... | collective-permute-start | bytes 196616 | tf_op jit(solution)/shard_map/ppermute | solution.py:54
where the time goes:
time: 162 us; the launch traced here: 161 us
  blocking collectives  51.2 us (32%)
  waiting for transfers between devices  46 us (28%)
  starting transfers between devices  24.8 us (15%)
  Pallas kernels  19.5 us (12%)
  local copies, waits for them, and re-layouts  10.7 us (7%)
  other arithmetic  8.24 us (5%)
    all_to_all x2, blocking collectives, remap(): planes = lax.all_to_all(blocks, 'azi', 0, 0, tiled=True)  30.7 us
    all_to_all x1, blocking collectives, remap(): blocks = lax.all_to_all(planes, 'azi', 0, 0, tiled=True)  20.5 us
    pallas_call x2, Pallas kernels, taylor(): pl.pallas_call(taylor_kernel, out_shape=jax.ShapeDtypeStruct(wide_state.s...  19.5 us
    ppermute x2, waiting for transfers between devices, extended(): lax.ppermute(cells[:, :, count - depth:, :], 'azi', ring('azi', 1))  15.2 us
    all_to_all x1, waiting for transfers between devices, remap(): blocks = lax.all_to_all(planes, 'azi', 0, 0, tiled=True)  11.2 us
    ppermute x2, starting transfers between devices, extended(): lax.ppermute(cells[:, :, :depth, :], 'azi', ring('azi', -1))  10.9 us
    ppermute x2, waiting for transfers between devices, extended(): low = jnp.swapaxes(lax.ppermute(low, 'rad', ring('rad', 1)), 2, 3)  8.67 us
    all_to_all x1, starting transfers between devices, remap(): blocks = lax.all_to_all(planes, 'azi', 0, 0, tiled=True)  8.35 us
  transfers between devices with their start and end apart: 9, of which 9 were waited for; matrix products, arithmetic and copies ran while one was open for 1% of the time, Pallas kernels for 0%

commit v1 on v0

--- a/solution.py
+++ b/solution.py
@@ -38,9 +38,9 @@
     ) / 12.0
 
 
-def extended(cells, depth):
+def azimuthal_halos(cells, depth):
     count = cells.shape[2]
-    cells = jnp.concatenate(
+    return jnp.concatenate(
         [
             lax.ppermute(cells[:, :, count - depth:, :], "azi", ring("azi", 1)),
             cells,
@@ -48,12 +48,19 @@
         ],
         axis=2,
     )
+
+
+def radial_halos(cells, depth):
     rows = cells.shape[3]
     low = jnp.swapaxes(cells[..., rows - depth:], 2, 3)
     high = jnp.swapaxes(cells[..., :depth], 2, 3)
     low = jnp.swapaxes(lax.ppermute(low, "rad", ring("rad", 1)), 2, 3)
     high = jnp.swapaxes(lax.ppermute(high, "rad", ring("rad", -1)), 2, 3)
     return jnp.concatenate([low, cells, high], axis=3)
+
+
+def extended(cells, depth):
+    return radial_halos(azimuthal_halos(cells, depth), depth)
 
 
 def inside_rows(start, extent, depth, row_count):
@@ -177,7 +184,7 @@
     return blocks
 
 
-def remap(state, offsets):
+def remap(state, offsets, depth):
     fields, levels, cells, rows = state.shape
     peers = lax.axis_size("azi")
     planes = state.reshape(peers, fields * levels // peers, cells, rows)
@@ -186,8 +193,14 @@
     for bit_pos in range((total - 1).bit_length()):
         chosen = (offsets >> bit_pos) & 1 == 1
         blocks = jnp.where(chosen, roll_cells(blocks, 1 << bit_pos), blocks)
+    if depth:
+        blocks = jnp.concatenate(
+            [jnp.roll(blocks, 1, axis=0)[:, :, cells - depth:], blocks,
+             jnp.roll(blocks, -1, axis=0)[:, :, :depth]],
+            axis=2,
+        )
     planes = lax.all_to_all(blocks, "azi", 0, 0, tiled=True)
-    return planes.reshape(fields, levels, cells, rows)
+    return planes.reshape(fields, levels, cells + 2 * depth, rows)
 
 
 def per_device(gas_state, sound_sq, offsets):
@@ -196,10 +209,11 @@
     wide = extended(jnp.concatenate([gas_state, sound_sq[None]]), depth)
     wide_state, wide_sound = wide[:4], wide[4]
     for timestep in range(STEPS):
-        if timestep:
-            wide_state = extended(state, depth)
         running = taylor(wide_state, wide_sound, depth, cells, row_count)
-        state = remap(running, offsets)
+        last = timestep == STEPS - 1
+        state = remap(running, offsets, 0 if last else depth)
+        if not last:
+            wide_state = radial_halos(state, depth)
     return state
 
 

time: 162 us -> 154 us (0.951)
  waiting for transfers between devices: 46 us -> 37 us
  starting transfers between devices: 24.8 us -> 19.7 us
  blocking collectives: 51.2 us -> 55.2 us
  local copies, waits for them, and re-layouts: 10.7 us -> 12.5 us
    ppermute x8 -> x6, waiting for transfers between devices: 34.9 us -> 25.9 us  [the longest x1 8.47 us: azimuthal_halos(): lax.ppermute(cells[:, :, count - depth:, :], 'azi', ring('azi', 1))]
    all_to_all x2, blocking collectives: 30.7 us -> 36.8 us  [remap(): planes = lax.all_to_all(blocks, 'azi', 0, 0, tiled=True)]
    ppermute x8 -> x6, starting transfers between devices: 16.5 us -> 11.3 us  [the longest x1 4.73 us: azimuthal_halos(): lax.ppermute(cells[:, :, :depth, :], 'azi', ring('azi', -1))]
    all_to_all x1, blocking collectives: 20.5 us -> 18.4 us  [remap(): blocks = lax.all_to_all(planes, 'azi', 0, 0, tiled=True)]
  transfers between devices with their start and end apart: 9 -> 7, of which waited for: 9 -> 7; matrix products, arithmetic and copies ran while one was open for 1% -> 1% of each run, Pallas kernels for 0% -> 0%
where the time goes in v1:
time: 154 us; the launch traced here: 153 us
  blocking collectives  55.2 us (36%)
  waiting for transfers between devices  37 us (24%)
  starting transfers between devices  19.7 us (13%)
  Pallas kernels  19.5 us (13%)
  local copies, waits for them, and re-layouts  12.5 us (8%)
  other arithmetic  8.52 us (6%)
    all_to_all x2, blocking collectives, remap(): planes = lax.all_to_all(blocks, 'azi', 0, 0, tiled=True)  36.8 us
    pallas_call x2, Pallas kernels, taylor(): pl.pallas_call(taylor_kernel, out_shape=jax.ShapeDtypeStruct(wide_state.s...  19.5 us
    all_to_all x1, blocking collectives, remap(): blocks = lax.all_to_all(planes, 'azi', 0, 0, tiled=True)  18.4 us
    all_to_all x1, waiting for transfers between devices, remap(): blocks = lax.all_to_all(planes, 'azi', 0, 0, tiled=True)  11.2 us
    ppermute x1, waiting for transfers between devices, azimuthal_halos(): lax.ppermute(cells[:, :, count - depth:, :], 'azi', ring('azi', 1))  8.47 us
    all_to_all x1, starting transfers between devices, remap(): blocks = lax.all_to_all(planes, 'azi', 0, 0, tiled=True)  8.35 us
    ppermute x2, waiting for transfers between devices, radial_halos(): low = jnp.swapaxes(lax.ppermute(low, 'rad', ring('rad', 1)), 2, 3)  7.96 us
    ppermute x2, waiting for transfers between devices, radial_halos(): high = jnp.swapaxes(lax.ppermute(high, 'rad', ring('rad', -1)), 2, 3)  7.16 us
  transfers between devices with their start and end apart: 7, of which 7 were waited for; matrix products, arithmetic and copies ran while one was open for 1% of the time, Pallas kernels for 0%

profile of v1, /device:TPU:64, one launch (start us, length us, event | category | flops | bytes accessed | tf_op | source)
XLA Modules:
  0.0 153.0 jit_solution(11476663324675129813)
XLA Ops:
  0.0 1.1 fusion.29
  1.1 2.0 %collective-permute-start = (f32[5,16,8,128]{3,2,1,0:T(8,128)S(1)}, f32[5,16,8,128]{3,2,1,0:T(8,128)S(1)}, u32[]{:S(2)}, u32[]{:S(2)}) collective-permute-start(f32[5,16,8,128]{3,2,1,0:T(8,128)S(1)} %get-tuple-element.9), channel_id=1, source_target_pairs={{0,1},{1,2},{2,3},{3,4},{4,5},{5,6},{6,7},{7,8},{8,9},{9,10},{10,1... | collective-permute-start | bytes 983048 | tf_op jit(solution)/shard_map/ppermute | solution.py:45
  3.1 4.7 %collective-permute-start.1 = (f32[5,16,8,128]{3,2,1,0:T(8,128)S(1)}, f32[5,16,8,128]{3,2,1,0:T(8,128)S(1)}, u32[]{:S(2)}, u32[]{:S(2)}) collective-permute-start(f32[5,16,8,128]{3,2,1,0:T(8,128)S(1)} %get-tuple-element.10), channel_id=1, source_target_pairs={{0,31},{1,0},{2,1},{3,2},{4,3},{5,4},{6,5},{7,6},{8,7},{9,8},{10,9... | collective-permute-start | bytes 983048 | tf_op jit(solution)/shard_map/ppermute | solution.py:47
  7.8 8.5 %collective-permute-done = f32[5,16,8,128]{3,2,1,0:T(8,128)S(1)} collective-permute-done((f32[5,16,8,128]{3,2,1,0:T(8,128)S(1)}, f32[5,16,8,128]{3,2,1,0:T(8,128)S(1)}, u32[]{:S(2)}, u32[]{:S(2)}) %collective-permute-start) | collective-permute-done | bytes 327712 | tf_op jit(solution)/shard_map/ppermute | solution.py:45
  16.3 2.3 %collective-permute-done.1 = f32[5,16,8,128]{3,2,1,0:T(8,128)S(1)} collective-permute-done((f32[5,16,8,128]{3,2,1,0:T(8,128)S(1)}, f32[5,16,8,128]{3,2,1,0:T(8,128)S(1)}, u32[]{:S(2)}, u32[]{:S(2)}) %collective-permute-start.1) | collective-permute-done | bytes 327712 | tf_op jit(solution)/shard_map/ppermute | solution.py:47
  18.6 1.4 pad_maximum_fusion
  19.9 0.5 slice_bitcast_fusion.1
  20.4 1.1 copy.4
  21.9 2.7 %collective-permute-start.3 = (f32[5,16,8,32]{3,2,1,0:T(8,128)S(1)}, f32[5,16,8,32]{3,2,1,0:T(8,128)}, u32[]{:S(2)}, u32[]{:S(2)}) collective-permute-start(f32[5,16,8,32]{3,2,1,0:T(8,128)S(1)} %copy.6), channel_id=1, source_target_pairs={{0,224},{32,0},{64,32},{96,64},{128,96},{160,128},{192,160},{224,1... | collective-permute-start | bytes 245768 | tf_op jit(solution)/shard_map/ppermute | solution.py:58
  24.6 5.2 %collective-permute-done.2 = f32[5,16,8,32]{3,2,1,0:T(8,128)S(1)} collective-permute-done((f32[5,16,8,32]{3,2,1,0:T(8,128)}, f32[5,16,8,32]{3,2,1,0:T(8,128)S(1)}, u32[]{:S(2)}, u32[]{:S(2)}) %collective-permute-start.2) | collective-permute-done | bytes 81952 | tf_op jit(solution)/shard_map/ppermute | solution.py:57
  29.8 0.4 copy.5
  30.2 2.5 %collective-permute-done.3 = f32[5,16,8,32]{3,2,1,0:T(8,128)} collective-permute-done((f32[5,16,8,32]{3,2,1,0:T(8,128)S(1)}, f32[5,16,8,32]{3,2,1,0:T(8,128)}, u32[]{:S(2)}, u32[]{:S(2)}) %collective-permute-start.3) | collective-permute-done | bytes 81952 | tf_op jit(solution)/shard_map/ppermute | solution.py:58
  32.8 1.4 copy.7
  34.2 1.3 maximum_bitcast_fusion
  35.6 0.9 fusion.7.state_ref
  36.5 9.7 %shard_map.37 = f32[4,16,32,256]{3,2,1,0:T(8,128)S(1)} custom-call(f32[1,256]{1,0:T(1,128)S(1)} %and_convert_fusion.keep_ref, f32[16,32,256]{2,1,0:T(8,128)S(1)} %pad.12.sound_ref, f32[4,16,32,256]{3,2,1,0:T(8,128)S(1)} %fusion.7.state_ref), custom_call_target="tpu_custom_call" | custom-call | flops 125829120 | bytes 4718592 | tf_op jit(solution)/shard_map/pallas_call | solution.py:160
  46.3 1.0 slice.288
  47.2 8.4 %all-to-all-start = ((f32[32,2,16,128]{3,2,1,0:T(8,128)}), f32[32,2,16,128]{3,2,1,0:T(8,128)S(1)}, u32[]{:S(2)}, u32[]{:S(2)}) async-start(f32[32,2,16,128]{3,2,1,0:T(8,128)} %bitcast.6), calls=%async_computation | async-start | bytes 1048576 | tf_op jit(solution)/shard_map/all_to_all | solution.py:191
  55.6 11.2 %all-to-all-done = f32[32,2,16,128]{3,2,1,0:T(8,128)S(1)} async-done(((f32[32,2,16,128]{3,2,1,0:T(8,128)}), f32[32,2,16,128]{3,2,1,0:T(8,128)S(1)}, u32[]{:S(2)}, u32[]{:S(2)}) %all-to-all-start) | async-done | bytes 524320 | tf_op jit(solution)/shard_map/all_to_all | solution.py:191
  68.5 20.8 %all_to_all.20 = f32[32,2,32,128]{3,2,1,0:T(8,128)S(1)} all-to-all(f32[32,2,32,128]{3,2,1,0:T(8,128)S(1)} %fusion.11), channel_id=1, replica_groups=mesh['rad'=8,'azi'=32] {'azi'}, dimensions={0} | all-to-all | bytes 2097152 | tf_op jit(solution)/shard_map/all_to_all | solution.py:202
  89.2 1.3 slice_bitcast_fusion.3
  90.6 1.5 %copy.10 = f32[4,16,8,32]{3,2,1,0:T(8,128)S(1)} copy(f32[4,16,8,32]{2,3,1,0:T(8,128)} %get-tuple-element.8) | data formatting | bytes 131072 | tf_op jit(solution)/shard_map/transpose | solution.py:56
  92.1 0.5 collective-permute-start.5
  93.0 1.4 collective-permute-start.4
  94.3 4.6 %collective-permute-done.5 = f32[4,16,8,32]{3,2,1,0:T(8,128)S(1)} collective-permute-done((f32[4,16,8,32]{3,2,1,0:T(8,128)S(1)}, f32[4,16,8,32]{3,2,1,0:T(8,128)S(1)}, u32[]{:S(2)}, u32[]{:S(2)}) %collective-permute-start.5) | collective-permute-done | bytes 65568 | tf_op jit(solution)/shard_map/ppermute | solution.py:58
  99.3 2.8 %collective-permute-done.4 = f32[4,16,8,32]{3,2,1,0:T(8,128)} collective-permute-done((f32[4,16,8,32]{3,2,1,0:T(8,128)S(1)}, f32[4,16,8,32]{3,2,1,0:T(8,128)}, u32[]{:S(2)}, u32[]{:S(2)}) %collective-permute-start.4) | collective-permute-done | bytes 65568 | tf_op jit(solution)/shard_map/ppermute | solution.py:57
  102.1 2.3 %copy.9 = f32[4,16,8,32]{2,3,1,0:T(8,128)} copy(f32[4,16,8,32]{3,2,1,0:T(8,128)} %collective-permute-done.4) | data formatting | bytes 131072 | tf_op jit(solution)/shard_map/ppermute | solution.py:57
  104.4 2.1 %select_maximum_fusion.state_ref = f32[4,16,32,256]{3,2,1,0:T(8,128)S(1)} fusion(f32[4,16,32,8]{3,2,1,0:T(8,128)S(1)} %bitcast.37, f32[4,16,32,128]{3,2,1,0:T(8,128)S(1)} %bitcast.26, f32[4,16,32,8]{3,2,1,0:T(8,128)} %bitcast.38), kind=kLoop, calls=%fused_computation | loop fusion | flops 3145728 | bytes 3276800 | tf_op jit(solution)/shard_map/concatenate | solution.py:59
  106.5 9.7 %shard_map.38 = f32[4,16,32,256]{3,2,1,0:T(8,128)S(1)} custom-call(f32[1,256]{1,0:T(1,128)S(1)} %and_convert_fusion.keep_ref, f32[16,32,256]{2,1,0:T(8,128)S(1)} %pad.12.sound_ref, f32[4,16,32,256]{3,2,1,0:T(8,128)S(1)} %select_maximum_fusion.state_ref), custom_call_target="tpu_custom_call" | custom-call | flops 125829120 | bytes 4718592 | tf_op jit(solution)/shard_map/pallas_call | solution.py:160
  116.5 18.4 %all_to_all.21 = f32[32,2,16,128]{3,2,1,0:T(8,128)S(1)} all-to-all(f32[32,2,16,128]{3,2,1,0:T(8,128)S(1)} %bitcast.43), channel_id=1, replica_groups=mesh['rad'=8,'azi'=32] {'azi'}, dimensions={0} | all-to-all | bytes 1048576 | tf_op jit(solution)/shard_map/all_to_all | solution.py:191
  136.3 16.0 %all_to_all.22 = f32[32,2,16,128]{3,2,1,0:T(8,128)S(1)} all-to-all(f32[32,2,16,128]{3,2,1,0:T(8,128)S(1)} %maximum_select_fusion.9), channel_id=1, replica_groups=mesh['rad'=8,'azi'=32] {'azi'}, dimensions={0} | all-to-all | bytes 1048576 | tf_op jit(solution)/shard_map/all_to_all | solution.py:202
  152.2 0.8 copy.13
  (77 shorter events, 4.0 us)
Async XLA Ops:
  1.1 15.2 %collective-permute-start = (f32[5,16,8,128]{3,2,1,0:T(8,128)S(1)}, f32[5,16,8,128]{3,2,1,0:T(8,128)S(1)}, u32[]{:S(2)}, u32[]{:S(2)}) collective-permute-start(f32[5,16,8,128]{3,2,1,0:T(8,128)S(1)} %get-tuple-element.9), channel_id=1, source_target_pairs={{0,1},{1,2},{2,3},{3,4},{4,5},{5,6},{6,7},{7,8},{8,9},{9,10},{10,1... | collective-permute-start | bytes 983048 | tf_op jit(solution)/shard_map/ppermute | solution.py:45
  3.1 15.5 %collective-permute-start.1 = (f32[5,16,8,128]{3,2,1,0:T(8,128)S(1)}, f32[5,16,8,128]{3,2,1,0:T(8,128)S(1)}, u32[]{:S(2)}, u32[]{:S(2)}) collective-permute-start(f32[5,16,8,128]{3,2,1,0:T(8,128)S(1)} %get-tuple-element.10), channel_id=1, source_target_pairs={{0,31},{1,0},{2,1},{3,2},{4,3},{5,4},{6,5},{7,6},{8,7},{9,8},{10,9... | collective-permute-start | bytes 983048 | tf_op jit(solution)/shard_map/ppermute | solution.py:47
  18.6 1.8 %copy-start.2 = (f32[5,16,8,128]{3,2,1,0:T(8,128)}, f32[5,16,8,128]{3,2,1,0:T(8,128)S(1)}, u32[]{:S(2)}) copy-start(f32[5,16,8,128]{3,2,1,0:T(8,128)S(1)} %collective-permute-done.1) | copy-start | bytes 983044
  21.5 8.3 %collective-permute-start.2 = (f32[5,16,8,32]{3,2,1,0:T(8,128)}, f32[5,16,8,32]{3,2,1,0:T(8,128)S(1)}, u32[]{:S(2)}, u32[]{:S(2)}) collective-permute-start(f32[5,16,8,32]{3,2,1,0:T(8,128)} %copy.4), channel_id=1, source_target_pairs={{0,32},{32,64},{64,96},{96,128},{128,160},{160,192},{192,224},{224... | collective-permute-start | bytes 245768 | tf_op jit(solution)/shard_map/ppermute | solution.py:57
  21.5 12.6 %copy-start = (f32[4,16,16,128]{3,2,1,0:T(8,128)S(1)}, f32[4,16,16,128]{3,2,1,0:T(8,128)}, u32[]{:S(2)}) copy-start(f32[4,16,16,128]{3,2,1,0:T(8,128)} %param.3) | copy-start | bytes 1572868
  21.9 10.8 %collective-permute-start.3 = (f32[5,16,8,32]{3,2,1,0:T(8,128)S(1)}, f32[5,16,8,32]{3,2,1,0:T(8,128)}, u32[]{:S(2)}, u32[]{:S(2)}) collective-permute-start(f32[5,16,8,32]{3,2,1,0:T(8,128)S(1)} %copy.6), channel_id=1, source_target_pairs={{0,224},{32,0},{64,32},{96,64},{128,96},{160,128},{192,160},{224,1... | collective-permute-start | bytes 245768 | tf_op jit(solution)/shard_map/ppermute | solution.py:58
  34.2 1.4 copy-start.1
  34.2 1.4 copy-start.3
  34.2 1.4 copy-start.4
  46.2 9.4 %copy-start.5 = (s32[128]{0:T(128)S(1)}, s32[128]{0:T(128)}, u32[]{:S(2)}) copy-start(s32[128]{0:T(128)} %param.5) | copy-start | bytes 1540
  47.2 19.6 %all-to-all-start = ((f32[32,2,16,128]{3,2,1,0:T(8,128)}), f32[32,2,16,128]{3,2,1,0:T(8,128)S(1)}, u32[]{:S(2)}, u32[]{:S(2)}) async-start(f32[32,2,16,128]{3,2,1,0:T(8,128)} %bitcast.6), calls=%async_computation | async-start | bytes 1048576 | tf_op jit(solution)/shard_map/all_to_all | solution.py:191
  92.1 6.8 %collective-permute-start.5 = (f32[4,16,8,32]{3,2,1,0:T(8,128)S(1)}, f32[4,16,8,32]{3,2,1,0:T(8,128)S(1)}, u32[]{:S(2)}, u32[]{:S(2)}) collective-permute-start(f32[4,16,8,32]{3,2,1,0:T(8,128)S(1)} %copy.10), channel_id=1, source_target_pairs={{0,224},{32,0},{64,32},{96,64},{128,96},{160,128},{192,160},{224,1... | collective-permute-start | bytes 196616 | tf_op jit(solution)/shard_map/ppermute | solution.py:58
  93.0 9.1 %collective-permute-start.4 = (f32[4,16,8,32]{3,2,1,0:T(8,128)S(1)}, f32[4,16,8,32]{3,2,1,0:T(8,128)}, u32[]{:S(2)}, u32[]{:S(2)}) collective-permute-start(f32[4,16,8,32]{3,2,1,0:T(8,128)S(1)} %copy.8), channel_id=1, source_target_pairs={{0,32},{32,64},{64,96},{96,128},{128,160},{160,192},{192,224},{224... | collective-permute-start | bytes 196616 | tf_op jit(solution)/shard_map/ppermute | solution.py:57

commit v2 on v1

--- a/solution.py
+++ b/solution.py
@@ -56,17 +56,19 @@
     high = jnp.swapaxes(cells[..., :depth], 2, 3)
     low = jnp.swapaxes(lax.ppermute(low, "rad", ring("rad", 1)), 2, 3)
     high = jnp.swapaxes(lax.ppermute(high, "rad", ring("rad", -1)), 2, 3)
-    return jnp.concatenate([low, cells, high], axis=3)
+    lanes = 128 * -(-(rows + 2 * depth) // 128)
+    unused = jnp.zeros(cells.shape[:3] + (lanes - rows - 2 * depth,), cells.dtype)
+    return jnp.concatenate([cells, high, unused, low], axis=3)
 
 
 def extended(cells, depth):
     return radial_halos(azimuthal_halos(cells, depth), depth)
 
 
-def inside_rows(start, extent, depth, row_count):
-    global_row = (
-        lax.axis_index("rad") * row_count - depth + start + jnp.arange(extent, dtype=jnp.int32)
-    )
+def inside_rows(lanes, depth, row_count):
+    lane = jnp.arange(lanes, dtype=jnp.int32)
+    lane = jnp.where(lane >= lanes - depth, lane - lanes, lane)
+    global_row = lax.axis_index("rad") * row_count + lane
     return (global_row >= 0) & (global_row < row_count * lax.axis_size("rad"))
 
 
@@ -150,11 +152,7 @@
 
 
 def taylor(wide_state, wide_sound, depth, cells, row_count):
-    lanes = 128 * -(-wide_state.shape[3] // 128)
-    extra = lanes - wide_state.shape[3]
-    wide_state = jnp.pad(wide_state, ((0, 0), (0, 0), (0, 0), (0, extra)))
-    wide_sound = jnp.pad(wide_sound, ((0, 0), (0, 0), (0, extra)))
-    keep = inside_rows(0, lanes, depth, row_count).astype(jnp.float32)[None, :]
+    keep = inside_rows(wide_state.shape[3], depth, row_count).astype(jnp.float32)[None, :]
     whole = pl.BlockSpec(memory_space=pltpu.VMEM)
     size = wide_state.size
     running = pl.pallas_call(
@@ -168,7 +166,7 @@
             flops=60 * ORDER * size, transcendentals=0, bytes_accessed=4 * (2 * size + size // 4)
         ),
     )(keep, wide_sound, wide_state)
-    return running[:, :, depth:depth + cells, depth:depth + row_count]
+    return running[:, :, depth:depth + cells, :row_count]
 
 
 def roll_cells(blocks, shift):

time: 154 us -> 153 us (level)
  blocking collectives: 55.2 us -> 53.3 us
    all_to_all x1, starting transfers between devices: 8.35 us -> 11 us  [remap(): blocks = lax.all_to_all(planes, 'azi', 0, 0, tiled=True)]
    ppermute x2, waiting for transfers between devices: 7.96 us -> 5.54 us  [radial_halos(): low = jnp.swapaxes(lax.ppermute(low, 'rad', ring('rad', 1)), 2, 3)]
    all_to_all x1, blocking collectives: 18.4 us -> 16.4 us  [remap(): blocks = lax.all_to_all(planes, 'azi', 0, 0, tiled=True)]
    all_to_all x1, waiting for transfers between devices: 11.2 us -> 13.2 us  [remap(): blocks = lax.all_to_all(planes, 'azi', 0, 0, tiled=True)]
    transpose x4 -> x2, local copies, waits for them, and re-layouts: 3.24 us -> 1.93 us  [radial_halos(): low = jnp.swapaxes(cells[..., rows - depth:], 2, 3)]
  transfers between devices with their start and end apart: 7 -> 7, of which waited for: 7 -> 6; matrix products, arithmetic and copies ran while one was open for 1% -> 1% of each run, Pallas kernels for 0% -> 0%
where the time goes in v2:
time: 153 us; the launch traced here: 151 us
  blocking collectives  53.3 us (35%)
  waiting for transfers between devices  37.3 us (24%)
  starting transfers between devices  21.1 us (14%)
  Pallas kernels  19.5 us (13%)
  local copies, waits for them, and re-layouts  12.4 us (8%)
  other arithmetic  7.28 us (5%)
    all_to_all x2, blocking collectives, remap(): planes = lax.all_to_all(blocks, 'azi', 0, 0, tiled=True)  36.9 us
    pallas_call x2, Pallas kernels, taylor(): pl.pallas_call(taylor_kernel, out_shape=jax.ShapeDtypeStruct(wide_state.s...  19.5 us
    all_to_all x1, blocking collectives, remap(): blocks = lax.all_to_all(planes, 'azi', 0, 0, tiled=True)  16.4 us
    all_to_all x1, waiting for transfers between devices, remap(): blocks = lax.all_to_all(planes, 'azi', 0, 0, tiled=True)  13.2 us
    all_to_all x1, starting transfers between devices, remap(): blocks = lax.all_to_all(planes, 'azi', 0, 0, tiled=True)  11 us
    ppermute x1, waiting for transfers between devices, azimuthal_halos(): lax.ppermute(cells[:, :, count - depth:, :], 'azi', ring('azi', 1))  8.39 us
    ppermute x2, waiting for transfers between devices, radial_halos(): high = jnp.swapaxes(lax.ppermute(high, 'rad', ring('rad', -1)), 2, 3)  7.89 us
    ppermute x2, waiting for transfers between devices, radial_halos(): low = jnp.swapaxes(lax.ppermute(low, 'rad', ring('rad', 1)), 2, 3)  5.54 us
  transfers between devices with their start and end apart: 7, of which 6 were waited for; matrix products, arithmetic and copies ran while one was open for 1% of the time, Pallas kernels for 0%

profile of v2, /device:TPU:64, one launch (start us, length us, event | category | flops | bytes accessed | tf_op | source)
XLA Modules:
  0.0 151.5 jit_solution(16360128166294158094)
XLA Ops:
  0.0 1.1 fusion.18
  1.1 2.0 %collective-permute-start = (f32[5,16,8,128]{3,2,1,0:T(8,128)S(1)}, f32[5,16,8,128]{3,2,1,0:T(8,128)S(1)}, u32[]{:S(2)}, u32[]{:S(2)}) collective-permute-start(f32[5,16,8,128]{3,2,1,0:T(8,128)S(1)} %get-tuple-element.9), channel_id=1, source_target_pairs={{0,1},{1,2},{2,3},{3,4},{4,5},{5,6},{6,7},{7,8},{8,9},{9,10},{10,1... | collective-permute-start | bytes 983048 | tf_op jit(solution)/shard_map/ppermute | solution.py:45
  3.1 4.7 %collective-permute-start.1 = (f32[5,16,8,128]{3,2,1,0:T(8,128)S(1)}, f32[5,16,8,128]{3,2,1,0:T(8,128)S(1)}, u32[]{:S(2)}, u32[]{:S(2)}) collective-permute-start(f32[5,16,8,128]{3,2,1,0:T(8,128)S(1)} %get-tuple-element.10), channel_id=1, source_target_pairs={{0,31},{1,0},{2,1},{3,2},{4,3},{5,4},{6,5},{7,6},{8,7},{9,8},{10,9... | collective-permute-start | bytes 983048 | tf_op jit(solution)/shard_map/ppermute | solution.py:47
  7.9 8.4 %collective-permute-done = f32[5,16,8,128]{3,2,1,0:T(8,128)S(1)} collective-permute-done((f32[5,16,8,128]{3,2,1,0:T(8,128)S(1)}, f32[5,16,8,128]{3,2,1,0:T(8,128)S(1)}, u32[]{:S(2)}, u32[]{:S(2)}) %collective-permute-start) | collective-permute-done | bytes 327712 | tf_op jit(solution)/shard_map/ppermute | solution.py:45
  16.3 2.3 %collective-permute-done.1 = f32[5,16,8,128]{3,2,1,0:T(8,128)S(1)} collective-permute-done((f32[5,16,8,128]{3,2,1,0:T(8,128)S(1)}, f32[5,16,8,128]{3,2,1,0:T(8,128)S(1)}, u32[]{:S(2)}, u32[]{:S(2)}) %collective-permute-start.1) | collective-permute-done | bytes 327712 | tf_op jit(solution)/shard_map/ppermute | solution.py:47
  18.6 0.7 copy-done.1
  19.3 1.2 pad_maximum_fusion.2
  20.5 0.5 slice_bitcast_fusion.1
  21.0 0.4 copy.4
  21.5 0.4 copy.6
  21.9 0.6 collective-permute-start.3
  22.4 7.1 %collective-permute-done.2 = f32[5,16,8,32]{3,2,1,0:T(8,128)S(1)} collective-permute-done((f32[5,16,8,32]{3,2,1,0:T(8,128)S(1)}, f32[5,16,8,32]{3,2,1,0:T(8,128)S(1)}, u32[]{:S(2)}, u32[]{:S(2)}) %collective-permute-start.2) | collective-permute-done | bytes 81952 | tf_op jit(solution)/shard_map/ppermute | solution.py:58
  29.6 0.4 copy.5
  30.0 1.4 copy.7
  31.4 1.5 %pad_maximum_fusion = f32[5,16,32,256]{3,2,1,0:T(8,128)S(1)} fusion(f32[5,16,32,8]{3,2,1,0:T(8,128)S(1)} %bitcast.34, f32[5,16,32,8]{3,2,1,0:T(8,128)S(1)} %bitcast.33, f32[5,16,8,128]{3,2,1,0:T(8,128)} %copy-done.1, f32[1,16,16,128]{3,2,1,0:T(8,128)} %bitcast.41, f32[4,16,16,128]{3,2,1,0:T(8,128)S(1)} %copy-done, ...), kind=kLoop, calls=%fused_computation | loop fusion | flops 3932160 | bytes 4097024 | tf_op jit(solution)/shard_map/concatenate | solution.py:61
  33.1 9.7 %shard_map.37 = f32[4,16,32,256]{3,2,1,0:T(8,128)S(1)} custom-call(f32[1,256]{1,0:T(1,128)S(1)} %and_convert_fusion.keep_ref, f32[16,32,256]{2,1,0:T(8,128)S(1)} %slice_bitcast_fusion.4.sound_ref, f32[4,16,32,256]{3,2,1,0:T(8,128)S(1)} %slice.289.state_ref), custom_call_target="tpu_custom_call" | custom-call | flops 125829120 | bytes 4718592 | tf_op jit(solution)/shard_map/pallas_call | solution.py:158
  42.9 0.8 slice.290
  43.7 11.0 %all-to-all-start = ((f32[32,2,16,128]{3,2,1,0:T(8,128)}), f32[32,2,16,128]{3,2,1,0:T(8,128)S(1)}, u32[]{:S(2)}, u32[]{:S(2)}) async-start(f32[32,2,16,128]{3,2,1,0:T(8,128)} %bitcast.6), calls=%async_computation | async-start | bytes 1048576 | tf_op jit(solution)/shard_map/all_to_all | solution.py:189
  54.7 13.2 %all-to-all-done = f32[32,2,16,128]{3,2,1,0:T(8,128)S(1)} async-done(((f32[32,2,16,128]{3,2,1,0:T(8,128)}), f32[32,2,16,128]{3,2,1,0:T(8,128)S(1)}, u32[]{:S(2)}, u32[]{:S(2)}) %all-to-all-start) | async-done | bytes 524320 | tf_op jit(solution)/shard_map/all_to_all | solution.py:189
  69.6 20.7 %all_to_all.20 = f32[32,2,32,128]{3,2,1,0:T(8,128)S(1)} all-to-all(f32[32,2,32,128]{3,2,1,0:T(8,128)S(1)} %fusion), channel_id=1, replica_groups=mesh['rad'=8,'azi'=32] {'azi'}, dimensions={0} | all-to-all | bytes 2097152 | tf_op jit(solution)/shard_map/all_to_all | solution.py:200
  90.3 1.4 slice_bitcast_fusion.3
  91.7 1.5 %copy.10 = f32[4,16,8,32]{3,2,1,0:T(8,128)S(1)} copy(f32[4,16,8,32]{2,3,1,0:T(8,128)} %get-tuple-element.8) | data formatting | bytes 131072 | tf_op jit(solution)/shard_map/transpose | solution.py:55
  93.6 2.7 %collective-permute-start.4 = (f32[4,16,8,32]{3,2,1,0:T(8,128)S(1)}, f32[4,16,8,32]{3,2,1,0:T(8,128)}, u32[]{:S(2)}, u32[]{:S(2)}) collective-permute-start(f32[4,16,8,32]{3,2,1,0:T(8,128)S(1)} %copy.8), channel_id=1, source_target_pairs={{0,224},{32,0},{64,32},{96,64},{128,96},{160,128},{192,160},{224,1... | collective-permute-start | bytes 196616 | tf_op jit(solution)/shard_map/ppermute | solution.py:58
  96.3 5.5 %collective-permute-done.5 = f32[4,16,8,32]{3,2,1,0:T(8,128)S(1)} collective-permute-done((f32[4,16,8,32]{3,2,1,0:T(8,128)S(1)}, f32[4,16,8,32]{3,2,1,0:T(8,128)S(1)}, u32[]{:S(2)}, u32[]{:S(2)}) %collective-permute-start.5) | collective-permute-done | bytes 65568 | tf_op jit(solution)/shard_map/ppermute | solution.py:57
  101.8 0.4 copy.11
  102.2 0.7 collective-permute-done.4
  102.9 2.3 %copy.9 = f32[4,16,8,32]{2,3,1,0:T(8,128)} copy(f32[4,16,8,32]{3,2,1,0:T(8,128)} %collective-permute-done.4) | data formatting | bytes 131072 | tf_op jit(solution)/shard_map/ppermute | solution.py:58
  105.2 1.6 %pad_maximum_fusion.1.state_ref = f32[4,16,32,256]{3,2,1,0:T(8,128)S(1)} fusion(f32[4,16,32,8]{3,2,1,0:T(8,128)S(1)} %bitcast.35, f32[4,16,32,8]{3,2,1,0:T(8,128)} %bitcast.36, f32[4,16,32,128]{3,2,1,0:T(8,128)S(1)} %bitcast.26, f32[256]{0:T(256)S(1)} %pad.68.clone), kind=kLoop, calls=%fused_computation.1 | loop fusion | flops 1572864 | bytes 3277824 | tf_op jit(solution)/shard_map/concatenate | solution.py:61
  106.9 9.7 %shard_map.38 = f32[4,16,32,256]{3,2,1,0:T(8,128)S(1)} custom-call(f32[1,256]{1,0:T(1,128)S(1)} %and_convert_fusion.keep_ref, f32[16,32,256]{2,1,0:T(8,128)S(1)} %slice_bitcast_fusion.4.sound_ref, f32[4,16,32,256]{3,2,1,0:T(8,128)S(1)} %pad_maximum_fusion.1.state_ref), custom_call_target="tpu_custom_call" | custom-call | flops 125829120 | bytes 4718592 | tf_op jit(solution)/shard_map/pallas_call | solution.py:158
  116.7 16.4 %all_to_all.21 = f32[32,2,16,128]{3,2,1,0:T(8,128)S(1)} all-to-all(f32[32,2,16,128]{3,2,1,0:T(8,128)S(1)} %bitcast.37), channel_id=1, replica_groups=mesh['rad'=8,'azi'=32] {'azi'}, dimensions={0} | all-to-all | bytes 1048576 | tf_op jit(solution)/shard_map/all_to_all | solution.py:189
  134.5 16.2 %all_to_all.22 = f32[32,2,16,128]{3,2,1,0:T(8,128)S(1)} all-to-all(f32[32,2,16,128]{3,2,1,0:T(8,128)S(1)} %maximum_select_fusion.9), channel_id=1, replica_groups=mesh['rad'=8,'azi'=32] {'azi'}, dimensions={0} | all-to-all | bytes 1048576 | tf_op jit(solution)/shard_map/all_to_all | solution.py:200
  150.7 0.8 copy.13
  (73 shorter events, 3.4 us)
Async XLA Ops:
  1.1 15.2 %collective-permute-start = (f32[5,16,8,128]{3,2,1,0:T(8,128)S(1)}, f32[5,16,8,128]{3,2,1,0:T(8,128)S(1)}, u32[]{:S(2)}, u32[]{:S(2)}) collective-permute-start(f32[5,16,8,128]{3,2,1,0:T(8,128)S(1)} %get-tuple-element.9), channel_id=1, source_target_pairs={{0,1},{1,2},{2,3},{3,4},{4,5},{5,6},{6,7},{7,8},{8,9},{9,10},{10,1... | collective-permute-start | bytes 983048 | tf_op jit(solution)/shard_map/ppermute | solution.py:45
  3.1 15.5 %collective-permute-start.1 = (f32[5,16,8,128]{3,2,1,0:T(8,128)S(1)}, f32[5,16,8,128]{3,2,1,0:T(8,128)S(1)}, u32[]{:S(2)}, u32[]{:S(2)}) collective-permute-start(f32[5,16,8,128]{3,2,1,0:T(8,128)S(1)} %get-tuple-element.10), channel_id=1, source_target_pairs={{0,31},{1,0},{2,1},{3,2},{4,3},{5,4},{6,5},{7,6},{8,7},{9,8},{10,9... | collective-permute-start | bytes 983048 | tf_op jit(solution)/shard_map/ppermute | solution.py:47
  18.6 0.7 copy-start.1
  21.4 8.2 %collective-permute-start.2 = (f32[5,16,8,32]{3,2,1,0:T(8,128)S(1)}, f32[5,16,8,32]{3,2,1,0:T(8,128)S(1)}, u32[]{:S(2)}, u32[]{:S(2)}) collective-permute-start(f32[5,16,8,32]{3,2,1,0:T(8,128)S(1)} %copy.4), channel_id=1, source_target_pairs={{0,224},{32,0},{64,32},{96,64},{128,96},{160,128},{192,160},{224,1... | collective-permute-start | bytes 245768 | tf_op jit(solution)/shard_map/ppermute | solution.py:58
  21.9 9.6 %copy-start = (f32[4,16,16,128]{3,2,1,0:T(8,128)S(1)}, f32[4,16,16,128]{3,2,1,0:T(8,128)}, u32[]{:S(2)}) copy-start(f32[4,16,16,128]{3,2,1,0:T(8,128)} %param.3) | copy-start | bytes 1572868
  21.9 8.1 %collective-permute-start.3 = (f32[5,16,8,32]{3,2,1,0:T(8,128)S(1)}, f32[5,16,8,32]{3,2,1,0:T(8,128)}, u32[]{:S(2)}, u32[]{:S(2)}) collective-permute-start(f32[5,16,8,32]{3,2,1,0:T(8,128)S(1)} %copy.6), channel_id=1, source_target_pairs={{0,32},{32,64},{64,96},{96,128},{128,160},{160,192},{192,224},{224... | collective-permute-start | bytes 245768 | tf_op jit(solution)/shard_map/ppermute | solution.py:57
  42.9 11.8 %copy-start.2 = (s32[128]{0:T(128)S(1)}, s32[128]{0:T(128)}, u32[]{:S(2)}) copy-start(s32[128]{0:T(128)} %param.5) | copy-start | bytes 1540
  43.7 24.2 %all-to-all-start = ((f32[32,2,16,128]{3,2,1,0:T(8,128)}), f32[32,2,16,128]{3,2,1,0:T(8,128)S(1)}, u32[]{:S(2)}, u32[]{:S(2)}) async-start(f32[32,2,16,128]{3,2,1,0:T(8,128)} %bitcast.6), calls=%async_computation | async-start | bytes 1048576 | tf_op jit(solution)/shard_map/all_to_all | solution.py:189
  93.2 8.6 %collective-permute-start.5 = (f32[4,16,8,32]{3,2,1,0:T(8,128)S(1)}, f32[4,16,8,32]{3,2,1,0:T(8,128)S(1)}, u32[]{:S(2)}, u32[]{:S(2)}) collective-permute-start(f32[4,16,8,32]{3,2,1,0:T(8,128)S(1)} %copy.10), channel_id=1, source_target_pairs={{0,32},{32,64},{64,96},{96,128},{128,160},{160,192},{192,224},{224... | collective-permute-start | bytes 196616 | tf_op jit(solution)/shard_map/ppermute | solution.py:57
  93.6 9.3 %collective-permute-start.4 = (f32[4,16,8,32]{3,2,1,0:T(8,128)S(1)}, f32[4,16,8,32]{3,2,1,0:T(8,128)}, u32[]{:S(2)}, u32[]{:S(2)}) collective-permute-start(f32[4,16,8,32]{3,2,1,0:T(8,128)S(1)} %copy.8), channel_id=1, source_target_pairs={{0,224},{32,0},{64,32},{96,64},{128,96},{160,128},{192,160},{224,1... | collective-permute-start | bytes 196616 | tf_op jit(solution)/shard_map/ppermute | solution.py:58

commit v3 on v2

--- a/solution.py
+++ b/solution.py
@@ -1,3 +1,5 @@
+import functools
+
 import jax
 import jax.numpy as jnp
 from jax import lax
@@ -108,9 +110,10 @@
     ) / 12.0
 
 
-def taylor_kernel(keep_ref, sound_ref, state_ref, running_ref, even_ref, odd_ref):
+def taylor_kernel(keep_ref, sound_ref, state_ref, running_ref, even_ref, odd_ref, own):
     keep = keep_ref[...] != 0.0
     levels = state_ref.shape[1]
+    first, cells, rows = own
 
     def start(level, carry):
         for field in range(4):
@@ -122,8 +125,11 @@
     lax.fori_loop(0, levels, start, 0)
     for degree in range(1, ORDER + 1):
         source, target = (even_ref, odd_ref) if degree % 2 else (odd_ref, even_ref)
-
-        def order(level, carry, source=source, target=target, scale=TIME_STEP / degree):
+        last = degree == ORDER
+        region = (slice(first, first + cells), slice(0, rows)) if last else (slice(None), slice(None))
+
+        def order(level, carry, source=source, target=target, scale=TIME_STEP / degree,
+                  last=last, region=region):
             near = [lax.rem(level + step + levels, levels) for step in (1, -1, 2, -2)]
 
             def vertical(value_at):
@@ -134,18 +140,24 @@
             azimuth_flow = source[2, level]
             pressure = sound_ref[level] * source[0, level]
             density_rate = -(
-                lane_diff(radial_flow)
-                + sublane_diff(azimuth_flow)
-                + vertical(lambda at: source[3, at])
+                lane_diff(radial_flow)[region]
+                + sublane_diff(azimuth_flow)[region]
+                + vertical(lambda at: source[3, at][region])
             )
-            radial_rate = -lane_diff(pressure) + 2.0 * ANGULAR_RATE * azimuth_flow
-            azimuth_rate = -sublane_diff(pressure) - (2.0 - SHEAR_RATE) * ANGULAR_RATE * radial_flow
-            vertical_rate = -vertical(lambda at: sound_ref[at] * source[0, at])
+            radial_rate = -lane_diff(pressure)[region] + 2.0 * ANGULAR_RATE * azimuth_flow[region]
+            azimuth_rate = -sublane_diff(pressure)[region] - (
+                2.0 - SHEAR_RATE
+            ) * ANGULAR_RATE * radial_flow[region]
+            vertical_rate = -vertical(lambda at: sound_ref[at][region] * source[0, at][region])
             rates = (density_rate, radial_rate, azimuth_rate, vertical_rate)
+            inside = keep[:, region[1]]
             for field, rate in enumerate(rates):
-                series = jnp.where(keep, scale * rate, 0.0)
-                target[field, level] = series
-                running_ref[field, level] = running_ref[field, level] + series
+                series = jnp.where(inside, scale * rate, 0.0)
+                if not last:
+                    target[field, level] = series
+                running_ref[field, level, region[0], region[1]] = (
+                    running_ref[field, level, region[0], region[1]] + series
+                )
             return carry
 
         lax.fori_loop(0, levels, order, 0)
@@ -156,7 +168,7 @@
     whole = pl.BlockSpec(memory_space=pltpu.VMEM)
     size = wide_state.size
     running = pl.pallas_call(
-        taylor_kernel,
+        functools.partial(taylor_kernel, own=(depth, cells, row_count)),
         out_shape=jax.ShapeDtypeStruct(wide_state.shape, jnp.float32),
         in_specs=[whole, whole, whole],
         out_specs=whole,

time: 153 us -> 152 us (level)
  no operation moved by 1% of the time
where the time goes in v3:
time: 152 us; the launch traced here: 150 us
  blocking collectives  53.3 us (35%)
  waiting for transfers between devices  37.3 us (25%)
  starting transfers between devices  21.1 us (14%)
  Pallas kernels  18.3 us (12%)
  local copies, waits for them, and re-layouts  12.4 us (8%)
  other arithmetic  7.28 us (5%)
    all_to_all x2, blocking collectives, remap(): planes = lax.all_to_all(blocks, 'azi', 0, 0, tiled=True)  36.9 us
    pallas_call x2, Pallas kernels, taylor(): pl.pallas_call(functools.partial(taylor_kernel, own=(depth, cells, row_co...  18.3 us
    all_to_all x1, blocking collectives, remap(): blocks = lax.all_to_all(planes, 'azi', 0, 0, tiled=True)  16.4 us
    all_to_all x1, waiting for transfers between devices, remap(): blocks = lax.all_to_all(planes, 'azi', 0, 0, tiled=True)  13.2 us
    all_to_all x1, starting transfers between devices, remap(): blocks = lax.all_to_all(planes, 'azi', 0, 0, tiled=True)  11 us
    ppermute x1, waiting for transfers between devices, azimuthal_halos(): lax.ppermute(cells[:, :, count - depth:, :], 'azi', ring('azi', 1))  8.39 us
    ppermute x2, waiting for transfers between devices, radial_halos(): high = jnp.swapaxes(lax.ppermute(high, 'rad', ring('rad', -1)), 2, 3)  7.89 us
    ppermute x2, waiting for transfers between devices, radial_halos(): low = jnp.swapaxes(lax.ppermute(low, 'rad', ring('rad', 1)), 2, 3)  5.54 us
  transfers between devices with their start and end apart: 7, of which 6 were waited for; matrix products, arithmetic and copies ran while one was open for 1% of the time, Pallas kernels for 0%

profile of v3, /device:TPU:64, one launch (start us, length us, event | category | flops | bytes accessed | tf_op | source)
XLA Modules:
  0.0 150.2 jit_solution(13425879259828941626)
XLA Ops:
  0.0 1.1 fusion.18
  1.1 2.0 %collective-permute-start = (f32[5,16,8,128]{3,2,1,0:T(8,128)S(1)}, f32[5,16,8,128]{3,2,1,0:T(8,128)S(1)}, u32[]{:S(2)}, u32[]{:S(2)}) collective-permute-start(f32[5,16,8,128]{3,2,1,0:T(8,128)S(1)} %get-tuple-element.9), channel_id=1, source_target_pairs={{0,1},{1,2},{2,3},{3,4},{4,5},{5,6},{6,7},{7,8},{8,9},{9,10},{10,1... | collective-permute-start | bytes 983048 | tf_op jit(solution)/shard_map/ppermute | solution.py:47
  3.1 4.7 %collective-permute-start.1 = (f32[5,16,8,128]{3,2,1,0:T(8,128)S(1)}, f32[5,16,8,128]{3,2,1,0:T(8,128)S(1)}, u32[]{:S(2)}, u32[]{:S(2)}) collective-permute-start(f32[5,16,8,128]{3,2,1,0:T(8,128)S(1)} %get-tuple-element.10), channel_id=1, source_target_pairs={{0,31},{1,0},{2,1},{3,2},{4,3},{5,4},{6,5},{7,6},{8,7},{9,8},{10,9... | collective-permute-start | bytes 983048 | tf_op jit(solution)/shard_map/ppermute | solution.py:49
  7.9 8.4 %collective-permute-done = f32[5,16,8,128]{3,2,1,0:T(8,128)S(1)} collective-permute-done((f32[5,16,8,128]{3,2,1,0:T(8,128)S(1)}, f32[5,16,8,128]{3,2,1,0:T(8,128)S(1)}, u32[]{:S(2)}, u32[]{:S(2)}) %collective-permute-start) | collective-permute-done | bytes 327712 | tf_op jit(solution)/shard_map/ppermute | solution.py:47
  16.3 2.3 %collective-permute-done.1 = f32[5,16,8,128]{3,2,1,0:T(8,128)S(1)} collective-permute-done((f32[5,16,8,128]{3,2,1,0:T(8,128)S(1)}, f32[5,16,8,128]{3,2,1,0:T(8,128)S(1)}, u32[]{:S(2)}, u32[]{:S(2)}) %collective-permute-start.1) | collective-permute-done | bytes 327712 | tf_op jit(solution)/shard_map/ppermute | solution.py:49
  18.6 0.7 copy-done.1
  19.3 1.2 pad_maximum_fusion.2
  20.5 0.5 slice_bitcast_fusion.1
  21.0 0.4 copy.4
  21.5 0.4 copy.6
  21.9 0.6 collective-permute-start.3
  22.4 7.1 %collective-permute-done.2 = f32[5,16,8,32]{3,2,1,0:T(8,128)S(1)} collective-permute-done((f32[5,16,8,32]{3,2,1,0:T(8,128)S(1)}, f32[5,16,8,32]{3,2,1,0:T(8,128)S(1)}, u32[]{:S(2)}, u32[]{:S(2)}) %collective-permute-start.2) | collective-permute-done | bytes 81952 | tf_op jit(solution)/shard_map/ppermute | solution.py:60
  29.6 0.4 copy.5
  30.0 1.4 copy.7
  31.4 1.5 %pad_maximum_fusion = f32[5,16,32,256]{3,2,1,0:T(8,128)S(1)} fusion(f32[5,16,32,8]{3,2,1,0:T(8,128)S(1)} %bitcast.34, f32[5,16,32,8]{3,2,1,0:T(8,128)S(1)} %bitcast.33, f32[5,16,8,128]{3,2,1,0:T(8,128)} %copy-done.1, f32[1,16,16,128]{3,2,1,0:T(8,128)} %bitcast.41, f32[4,16,16,128]{3,2,1,0:T(8,128)S(1)} %copy-done, ...), kind=kLoop, calls=%fused_computation | loop fusion | flops 3932160 | bytes 4097024 | tf_op jit(solution)/shard_map/concatenate | solution.py:63
  33.1 9.1 %shard_map.37 = f32[4,16,32,256]{3,2,1,0:T(8,128)S(1)} custom-call(f32[1,256]{1,0:T(1,128)S(1)} %and_convert_fusion.keep_ref, f32[16,32,256]{2,1,0:T(8,128)S(1)} %slice_bitcast_fusion.4.sound_ref, f32[4,16,32,256]{3,2,1,0:T(8,128)S(1)} %slice.289.state_ref), custom_call_target="tpu_custom_call" | custom-call | flops 125829120 | bytes 4718592 | tf_op jit(solution)/shard_map/pallas_call | solution.py:170
  42.3 0.8 slice.290
  43.1 11.0 %all-to-all-start = ((f32[32,2,16,128]{3,2,1,0:T(8,128)}), f32[32,2,16,128]{3,2,1,0:T(8,128)S(1)}, u32[]{:S(2)}, u32[]{:S(2)}) async-start(f32[32,2,16,128]{3,2,1,0:T(8,128)} %bitcast.6), calls=%async_computation | async-start | bytes 1048576 | tf_op jit(solution)/shard_map/all_to_all | solution.py:201
  54.1 13.2 %all-to-all-done = f32[32,2,16,128]{3,2,1,0:T(8,128)S(1)} async-done(((f32[32,2,16,128]{3,2,1,0:T(8,128)}), f32[32,2,16,128]{3,2,1,0:T(8,128)S(1)}, u32[]{:S(2)}, u32[]{:S(2)}) %all-to-all-start) | async-done | bytes 524320 | tf_op jit(solution)/shard_map/all_to_all | solution.py:201
  68.9 20.7 %all_to_all.20 = f32[32,2,32,128]{3,2,1,0:T(8,128)S(1)} all-to-all(f32[32,2,32,128]{3,2,1,0:T(8,128)S(1)} %fusion), channel_id=1, replica_groups=mesh['rad'=8,'azi'=32] {'azi'}, dimensions={0} | all-to-all | bytes 2097152 | tf_op jit(solution)/shard_map/all_to_all | solution.py:212
  89.7 1.4 slice_bitcast_fusion.3
  91.1 1.5 %copy.10 = f32[4,16,8,32]{3,2,1,0:T(8,128)S(1)} copy(f32[4,16,8,32]{2,3,1,0:T(8,128)} %get-tuple-element.8) | data formatting | bytes 131072 | tf_op jit(solution)/shard_map/transpose | solution.py:57
  93.0 2.7 %collective-permute-start.4 = (f32[4,16,8,32]{3,2,1,0:T(8,128)S(1)}, f32[4,16,8,32]{3,2,1,0:T(8,128)}, u32[]{:S(2)}, u32[]{:S(2)}) collective-permute-start(f32[4,16,8,32]{3,2,1,0:T(8,128)S(1)} %copy.8), channel_id=1, source_target_pairs={{0,224},{32,0},{64,32},{96,64},{128,96},{160,128},{192,160},{224,1... | collective-permute-start | bytes 196616 | tf_op jit(solution)/shard_map/ppermute | solution.py:60
  95.7 5.5 %collective-permute-done.5 = f32[4,16,8,32]{3,2,1,0:T(8,128)S(1)} collective-permute-done((f32[4,16,8,32]{3,2,1,0:T(8,128)S(1)}, f32[4,16,8,32]{3,2,1,0:T(8,128)S(1)}, u32[]{:S(2)}, u32[]{:S(2)}) %collective-permute-start.5) | collective-permute-done | bytes 65568 | tf_op jit(solution)/shard_map/ppermute | solution.py:59
  101.2 0.4 copy.11
  101.6 0.7 collective-permute-done.4
  102.3 2.3 %copy.9 = f32[4,16,8,32]{2,3,1,0:T(8,128)} copy(f32[4,16,8,32]{3,2,1,0:T(8,128)} %collective-permute-done.4) | data formatting | bytes 131072 | tf_op jit(solution)/shard_map/ppermute | solution.py:60
  104.6 1.6 %pad_maximum_fusion.1.state_ref = f32[4,16,32,256]{3,2,1,0:T(8,128)S(1)} fusion(f32[4,16,32,8]{3,2,1,0:T(8,128)S(1)} %bitcast.35, f32[4,16,32,8]{3,2,1,0:T(8,128)} %bitcast.36, f32[4,16,32,128]{3,2,1,0:T(8,128)S(1)} %bitcast.26, f32[256]{0:T(256)S(1)} %pad.68.clone), kind=kLoop, calls=%fused_computation.1 | loop fusion | flops 1572864 | bytes 3277824 | tf_op jit(solution)/shard_map/concatenate | solution.py:63
  106.3 9.1 %shard_map.38 = f32[4,16,32,256]{3,2,1,0:T(8,128)S(1)} custom-call(f32[1,256]{1,0:T(1,128)S(1)} %and_convert_fusion.keep_ref, f32[16,32,256]{2,1,0:T(8,128)S(1)} %slice_bitcast_fusion.4.sound_ref, f32[4,16,32,256]{3,2,1,0:T(8,128)S(1)} %pad_maximum_fusion.1.state_ref), custom_call_target="tpu_custom_call" | custom-call | flops 125829120 | bytes 4718592 | tf_op jit(solution)/shard_map/pallas_call | solution.py:170
  115.5 16.4 %all_to_all.21 = f32[32,2,16,128]{3,2,1,0:T(8,128)S(1)} all-to-all(f32[32,2,16,128]{3,2,1,0:T(8,128)S(1)} %bitcast.37), channel_id=1, replica_groups=mesh['rad'=8,'azi'=32] {'azi'}, dimensions={0} | all-to-all | bytes 1048576 | tf_op jit(solution)/shard_map/all_to_all | solution.py:201
  133.2 16.2 %all_to_all.22 = f32[32,2,16,128]{3,2,1,0:T(8,128)S(1)} all-to-all(f32[32,2,16,128]{3,2,1,0:T(8,128)S(1)} %maximum_select_fusion.9), channel_id=1, replica_groups=mesh['rad'=8,'azi'=32] {'azi'}, dimensions={0} | all-to-all | bytes 1048576 | tf_op jit(solution)/shard_map/all_to_all | solution.py:212
  149.4 0.8 copy.13
  (73 shorter events, 3.4 us)
Async XLA Ops:
  1.1 15.2 %collective-permute-start = (f32[5,16,8,128]{3,2,1,0:T(8,128)S(1)}, f32[5,16,8,128]{3,2,1,0:T(8,128)S(1)}, u32[]{:S(2)}, u32[]{:S(2)}) collective-permute-start(f32[5,16,8,128]{3,2,1,0:T(8,128)S(1)} %get-tuple-element.9), channel_id=1, source_target_pairs={{0,1},{1,2},{2,3},{3,4},{4,5},{5,6},{6,7},{7,8},{8,9},{9,10},{10,1... | collective-permute-start | bytes 983048 | tf_op jit(solution)/shard_map/ppermute | solution.py:47
  3.1 15.5 %collective-permute-start.1 = (f32[5,16,8,128]{3,2,1,0:T(8,128)S(1)}, f32[5,16,8,128]{3,2,1,0:T(8,128)S(1)}, u32[]{:S(2)}, u32[]{:S(2)}) collective-permute-start(f32[5,16,8,128]{3,2,1,0:T(8,128)S(1)} %get-tuple-element.10), channel_id=1, source_target_pairs={{0,31},{1,0},{2,1},{3,2},{4,3},{5,4},{6,5},{7,6},{8,7},{9,8},{10,9... | collective-permute-start | bytes 983048 | tf_op jit(solution)/shard_map/ppermute | solution.py:49
  18.6 0.7 copy-start.1
  21.4 8.2 %collective-permute-start.2 = (f32[5,16,8,32]{3,2,1,0:T(8,128)S(1)}, f32[5,16,8,32]{3,2,1,0:T(8,128)S(1)}, u32[]{:S(2)}, u32[]{:S(2)}) collective-permute-start(f32[5,16,8,32]{3,2,1,0:T(8,128)S(1)} %copy.4), channel_id=1, source_target_pairs={{0,224},{32,0},{64,32},{96,64},{128,96},{160,128},{192,160},{224,1... | collective-permute-start | bytes 245768 | tf_op jit(solution)/shard_map/ppermute | solution.py:60
  21.9 9.6 %copy-start = (f32[4,16,16,128]{3,2,1,0:T(8,128)S(1)}, f32[4,16,16,128]{3,2,1,0:T(8,128)}, u32[]{:S(2)}) copy-start(f32[4,16,16,128]{3,2,1,0:T(8,128)} %param.3) | copy-start | bytes 1572868
  21.9 8.1 %collective-permute-start.3 = (f32[5,16,8,32]{3,2,1,0:T(8,128)S(1)}, f32[5,16,8,32]{3,2,1,0:T(8,128)}, u32[]{:S(2)}, u32[]{:S(2)}) collective-permute-start(f32[5,16,8,32]{3,2,1,0:T(8,128)S(1)} %copy.6), channel_id=1, source_target_pairs={{0,32},{32,64},{64,96},{96,128},{128,160},{160,192},{192,224},{224... | collective-permute-start | bytes 245768 | tf_op jit(solution)/shard_map/ppermute | solution.py:59
  42.3 11.8 %copy-start.2 = (s32[128]{0:T(128)S(1)}, s32[128]{0:T(128)}, u32[]{:S(2)}) copy-start(s32[128]{0:T(128)} %param.5) | copy-start | bytes 1540
  43.1 24.2 %all-to-all-start = ((f32[32,2,16,128]{3,2,1,0:T(8,128)}), f32[32,2,16,128]{3,2,1,0:T(8,128)S(1)}, u32[]{:S(2)}, u32[]{:S(2)}) async-start(f32[32,2,16,128]{3,2,1,0:T(8,128)} %bitcast.6), calls=%async_computation | async-start | bytes 1048576 | tf_op jit(solution)/shard_map/all_to_all | solution.py:201
  92.6 8.6 %collective-permute-start.5 = (f32[4,16,8,32]{3,2,1,0:T(8,128)S(1)}, f32[4,16,8,32]{3,2,1,0:T(8,128)S(1)}, u32[]{:S(2)}, u32[]{:S(2)}) collective-permute-start(f32[4,16,8,32]{3,2,1,0:T(8,128)S(1)} %copy.10), channel_id=1, source_target_pairs={{0,32},{32,64},{64,96},{96,128},{128,160},{160,192},{192,224},{224... | collective-permute-start | bytes 196616 | tf_op jit(solution)/shard_map/ppermute | solution.py:59
  93.0 9.3 %collective-permute-start.4 = (f32[4,16,8,32]{3,2,1,0:T(8,128)S(1)}, f32[4,16,8,32]{3,2,1,0:T(8,128)}, u32[]{:S(2)}, u32[]{:S(2)}) collective-permute-start(f32[4,16,8,32]{3,2,1,0:T(8,128)S(1)} %copy.8), channel_id=1, source_target_pairs={{0,224},{32,0},{64,32},{96,64},{128,96},{160,128},{192,160},{224,1... | collective-permute-start | bytes 196616 | tf_op jit(solution)/shard_map/ppermute | solution.py:60

commit v4 on v3

--- a/solution.py
+++ b/solution.py
@@ -118,7 +118,7 @@
     def start(level, carry):
         for field in range(4):
             values = state_ref[field, level]
-            running_ref[field, level] = values
+            running_ref[field, level] = values[first:first + cells, :rows]
             even_ref[field, level] = jnp.where(keep, values, 0.0)
         return carry
 
@@ -155,9 +155,8 @@
                 series = jnp.where(inside, scale * rate, 0.0)
                 if not last:
                     target[field, level] = series
-                running_ref[field, level, region[0], region[1]] = (
-                    running_ref[field, level, region[0], region[1]] + series
-                )
+                own_part = series if last else series[first:first + cells, :rows]
+                running_ref[field, level] = running_ref[field, level] + own_part
             return carry
 
         lax.fori_loop(0, levels, order, 0)
@@ -169,7 +168,7 @@
     size = wide_state.size
     running = pl.pallas_call(
         functools.partial(taylor_kernel, own=(depth, cells, row_count)),
-        out_shape=jax.ShapeDtypeStruct(wide_state.shape, jnp.float32),
+        out_shape=jax.ShapeDtypeStruct(wide_state.shape[:2] + (cells, row_count), jnp.float32),
         in_specs=[whole, whole, whole],
         out_specs=whole,
         scratch_shapes=[pltpu.VMEM(wide_state.shape, jnp.float32)] * 2,
@@ -178,7 +177,7 @@
             flops=60 * ORDER * size, transcendentals=0, bytes_accessed=4 * (2 * size + size // 4)
         ),
     )(keep, wide_sound, wide_state)
-    return running[:, :, depth:depth + cells, :row_count]
+    return running
 
 
 def roll_cells(blocks, shift):

time: 152 us -> 152 us (level)
  no operation moved by 1% of the time
where the time goes in v4:
time: 152 us; the launch traced here: 150 us
  blocking collectives  53.3 us (35%)
  waiting for transfers between devices  37.3 us (25%)
  starting transfers between devices  21 us (14%)
  Pallas kernels  18.5 us (12%)
  local copies, waits for them, and re-layouts  11.6 us (8%)
  other arithmetic  7.28 us (5%)
    all_to_all x2, blocking collectives, remap(): planes = lax.all_to_all(blocks, 'azi', 0, 0, tiled=True)  36.9 us
    pallas_call x2, Pallas kernels, taylor(): pl.pallas_call(functools.partial(taylor_kernel, own=(depth, cells, row_co...  18.5 us
    all_to_all x1, blocking collectives, remap(): blocks = lax.all_to_all(planes, 'azi', 0, 0, tiled=True)  16.4 us
    all_to_all x1, waiting for transfers between devices, remap(): blocks = lax.all_to_all(planes, 'azi', 0, 0, tiled=True)  13.2 us
    all_to_all x1, starting transfers between devices, remap(): blocks = lax.all_to_all(planes, 'azi', 0, 0, tiled=True)  11 us
    ppermute x1, waiting for transfers between devices, azimuthal_halos(): lax.ppermute(cells[:, :, count - depth:, :], 'azi', ring('azi', 1))  8.39 us
    ppermute x2, waiting for transfers between devices, radial_halos(): high = jnp.swapaxes(lax.ppermute(high, 'rad', ring('rad', -1)), 2, 3)  7.89 us
    ppermute x2, waiting for transfers between devices, radial_halos(): low = jnp.swapaxes(lax.ppermute(low, 'rad', ring('rad', 1)), 2, 3)  5.54 us
  transfers between devices with their start and end apart: 7, of which 6 were waited for; matrix products, arithmetic and copies ran while one was open for 1% of the time, Pallas kernels for 0%

profile of v4, /device:TPU:64, one launch (start us, length us, event | category | flops | bytes accessed | tf_op | source)
XLA Modules:
  0.0 149.6 jit_solution(7976118849872298997)
XLA Ops:
  0.0 1.1 fusion.18
  1.1 2.0 %collective-permute-start = (f32[5,16,8,128]{3,2,1,0:T(8,128)S(1)}, f32[5,16,8,128]{3,2,1,0:T(8,128)S(1)}, u32[]{:S(2)}, u32[]{:S(2)}) collective-permute-start(f32[5,16,8,128]{3,2,1,0:T(8,128)S(1)} %get-tuple-element.9), channel_id=1, source_target_pairs={{0,1},{1,2},{2,3},{3,4},{4,5},{5,6},{6,7},{7,8},{8,9},{9,10},{10,1... | collective-permute-start | bytes 983048 | tf_op jit(solution)/shard_map/ppermute | solution.py:47
  3.1 4.7 %collective-permute-start.1 = (f32[5,16,8,128]{3,2,1,0:T(8,128)S(1)}, f32[5,16,8,128]{3,2,1,0:T(8,128)S(1)}, u32[]{:S(2)}, u32[]{:S(2)}) collective-permute-start(f32[5,16,8,128]{3,2,1,0:T(8,128)S(1)} %get-tuple-element.10), channel_id=1, source_target_pairs={{0,31},{1,0},{2,1},{3,2},{4,3},{5,4},{6,5},{7,6},{8,7},{9,8},{10,9... | collective-permute-start | bytes 983048 | tf_op jit(solution)/shard_map/ppermute | solution.py:49
  7.9 8.4 %collective-permute-done = f32[5,16,8,128]{3,2,1,0:T(8,128)S(1)} collective-permute-done((f32[5,16,8,128]{3,2,1,0:T(8,128)S(1)}, f32[5,16,8,128]{3,2,1,0:T(8,128)S(1)}, u32[]{:S(2)}, u32[]{:S(2)}) %collective-permute-start) | collective-permute-done | bytes 327712 | tf_op jit(solution)/shard_map/ppermute | solution.py:47
  16.3 2.3 %collective-permute-done.1 = f32[5,16,8,128]{3,2,1,0:T(8,128)S(1)} collective-permute-done((f32[5,16,8,128]{3,2,1,0:T(8,128)S(1)}, f32[5,16,8,128]{3,2,1,0:T(8,128)S(1)}, u32[]{:S(2)}, u32[]{:S(2)}) %collective-permute-start.1) | collective-permute-done | bytes 327712 | tf_op jit(solution)/shard_map/ppermute | solution.py:49
  18.6 0.7 copy-done.1
  19.3 1.2 pad_maximum_fusion.2
  20.5 0.5 slice_bitcast_fusion.1
  21.0 0.4 copy.4
  21.5 0.4 copy.6
  21.9 0.6 collective-permute-start.3
  22.4 7.1 %collective-permute-done.2 = f32[5,16,8,32]{3,2,1,0:T(8,128)S(1)} collective-permute-done((f32[5,16,8,32]{3,2,1,0:T(8,128)S(1)}, f32[5,16,8,32]{3,2,1,0:T(8,128)S(1)}, u32[]{:S(2)}, u32[]{:S(2)}) %collective-permute-start.2) | collective-permute-done | bytes 81952 | tf_op jit(solution)/shard_map/ppermute | solution.py:60
  29.6 0.4 copy.5
  30.0 1.4 copy.7
  31.4 1.5 %pad_maximum_fusion = f32[5,16,32,256]{3,2,1,0:T(8,128)S(1)} fusion(f32[5,16,32,8]{3,2,1,0:T(8,128)S(1)} %bitcast.35, f32[5,16,32,8]{3,2,1,0:T(8,128)S(1)} %bitcast.34, f32[5,16,8,128]{3,2,1,0:T(8,128)} %copy-done.1, f32[1,16,16,128]{3,2,1,0:T(8,128)} %bitcast.41, f32[4,16,16,128]{3,2,1,0:T(8,128)S(1)} %copy-done, ...), kind=kLoop, calls=%fused_computation | loop fusion | flops 3932160 | bytes 4097024 | tf_op jit(solution)/shard_map/concatenate | solution.py:63
  33.1 9.7 %shard_map.37 = f32[4,16,16,128]{3,2,1,0:T(8,128)} custom-call(f32[1,256]{1,0:T(1,128)S(1)} %and_convert_fusion.keep_ref, f32[16,32,256]{2,1,0:T(8,128)S(1)} %slice_bitcast_fusion.4.sound_ref, f32[4,16,32,256]{3,2,1,0:T(8,128)S(1)} %slice.281.state_ref), custom_call_target="tpu_custom_call" | custom-call | flops 125829120 | bytes 4718592 | tf_op jit(solution)/shard_map/pallas_call | solution.py:169
  42.8 11.0 %all-to-all-start = ((f32[32,2,16,128]{3,2,1,0:T(8,128)}), f32[32,2,16,128]{3,2,1,0:T(8,128)S(1)}, u32[]{:S(2)}, u32[]{:S(2)}) async-start(f32[32,2,16,128]{3,2,1,0:T(8,128)} %bitcast.6), calls=%async_computation | async-start | bytes 1048576 | tf_op jit(solution)/shard_map/all_to_all | solution.py:200
  53.8 13.2 %all-to-all-done = f32[32,2,16,128]{3,2,1,0:T(8,128)S(1)} async-done(((f32[32,2,16,128]{3,2,1,0:T(8,128)}), f32[32,2,16,128]{3,2,1,0:T(8,128)S(1)}, u32[]{:S(2)}, u32[]{:S(2)}) %all-to-all-start) | async-done | bytes 524320 | tf_op jit(solution)/shard_map/all_to_all | solution.py:200
  68.6 20.7 %all_to_all.20 = f32[32,2,32,128]{3,2,1,0:T(8,128)S(1)} all-to-all(f32[32,2,32,128]{3,2,1,0:T(8,128)S(1)} %fusion), channel_id=1, replica_groups=mesh['rad'=8,'azi'=32] {'azi'}, dimensions={0} | all-to-all | bytes 2097152 | tf_op jit(solution)/shard_map/all_to_all | solution.py:211
  89.4 1.4 slice_bitcast_fusion.3
  90.7 1.5 %copy.10 = f32[4,16,8,32]{3,2,1,0:T(8,128)S(1)} copy(f32[4,16,8,32]{2,3,1,0:T(8,128)} %get-tuple-element.8) | data formatting | bytes 131072 | tf_op jit(solution)/shard_map/transpose | solution.py:57
  92.4 0.3 copy.8
  92.7 2.7 %collective-permute-start.4 = (f32[4,16,8,32]{3,2,1,0:T(8,128)S(1)}, f32[4,16,8,32]{3,2,1,0:T(8,128)}, u32[]{:S(2)}, u32[]{:S(2)}) collective-permute-start(f32[4,16,8,32]{3,2,1,0:T(8,128)S(1)} %copy.8), channel_id=1, source_target_pairs={{0,224},{32,0},{64,32},{96,64},{128,96},{160,128},{192,160},{224,1... | collective-permute-start | bytes 196616 | tf_op jit(solution)/shard_map/ppermute | solution.py:60
  95.4 5.5 %collective-permute-done.5 = f32[4,16,8,32]{3,2,1,0:T(8,128)S(1)} collective-permute-done((f32[4,16,8,32]{3,2,1,0:T(8,128)S(1)}, f32[4,16,8,32]{3,2,1,0:T(8,128)S(1)}, u32[]{:S(2)}, u32[]{:S(2)}) %collective-permute-start.5) | collective-permute-done | bytes 65568 | tf_op jit(solution)/shard_map/ppermute | solution.py:59
  100.9 0.4 copy.11
  101.3 0.7 collective-permute-done.4
  102.0 2.3 %copy.9 = f32[4,16,8,32]{2,3,1,0:T(8,128)} copy(f32[4,16,8,32]{3,2,1,0:T(8,128)} %collective-permute-done.4) | data formatting | bytes 131072 | tf_op jit(solution)/shard_map/ppermute | solution.py:60
  104.3 1.6 %pad_maximum_fusion.1.state_ref = f32[4,16,32,256]{3,2,1,0:T(8,128)S(1)} fusion(f32[4,16,32,8]{3,2,1,0:T(8,128)S(1)} %bitcast.36, f32[4,16,32,8]{3,2,1,0:T(8,128)} %bitcast.37, f32[4,16,32,128]{3,2,1,0:T(8,128)S(1)} %bitcast.27, f32[256]{0:T(256)S(1)} %pad.68.clone), kind=kLoop, calls=%fused_computation.1 | loop fusion | flops 1572864 | bytes 3277824 | tf_op jit(solution)/shard_map/concatenate | solution.py:63
  106.0 8.9 %shard_map.38 = f32[4,16,16,128]{3,2,1,0:T(8,128)S(1)} custom-call(f32[1,256]{1,0:T(1,128)S(1)} %and_convert_fusion.keep_ref, f32[16,32,256]{2,1,0:T(8,128)S(1)} %slice_bitcast_fusion.4.sound_ref, f32[4,16,32,256]{3,2,1,0:T(8,128)S(1)} %pad_maximum_fusion.1.state_ref), custom_call_target="tpu_custom_call" | custom-call | flops 125829120 | bytes 4718592 | tf_op jit(solution)/shard_map/pallas_call | solution.py:169
  114.8 16.4 %all_to_all.21 = f32[32,2,16,128]{3,2,1,0:T(8,128)S(1)} all-to-all(f32[32,2,16,128]{3,2,1,0:T(8,128)S(1)} %bitcast.25), channel_id=1, replica_groups=mesh['rad'=8,'azi'=32] {'azi'}, dimensions={0} | all-to-all | bytes 1048576 | tf_op jit(solution)/shard_map/all_to_all | solution.py:200
  132.6 16.2 %all_to_all.22 = f32[32,2,16,128]{3,2,1,0:T(8,128)S(1)} all-to-all(f32[32,2,16,128]{3,2,1,0:T(8,128)S(1)} %maximum_select_fusion.9), channel_id=1, replica_groups=mesh['rad'=8,'azi'=32] {'azi'}, dimensions={0} | all-to-all | bytes 1048576 | tf_op jit(solution)/shard_map/all_to_all | solution.py:211
  148.8 0.8 copy.13
  (71 shorter events, 3.0 us)
Async XLA Ops:
  1.1 15.2 %collective-permute-start = (f32[5,16,8,128]{3,2,1,0:T(8,128)S(1)}, f32[5,16,8,128]{3,2,1,0:T(8,128)S(1)}, u32[]{:S(2)}, u32[]{:S(2)}) collective-permute-start(f32[5,16,8,128]{3,2,1,0:T(8,128)S(1)} %get-tuple-element.9), channel_id=1, source_target_pairs={{0,1},{1,2},{2,3},{3,4},{4,5},{5,6},{6,7},{7,8},{8,9},{9,10},{10,1... | collective-permute-start | bytes 983048 | tf_op jit(solution)/shard_map/ppermute | solution.py:47
  3.1 15.5 %collective-permute-start.1 = (f32[5,16,8,128]{3,2,1,0:T(8,128)S(1)}, f32[5,16,8,128]{3,2,1,0:T(8,128)S(1)}, u32[]{:S(2)}, u32[]{:S(2)}) collective-permute-start(f32[5,16,8,128]{3,2,1,0:T(8,128)S(1)} %get-tuple-element.10), channel_id=1, source_target_pairs={{0,31},{1,0},{2,1},{3,2},{4,3},{5,4},{6,5},{7,6},{8,7},{9,8},{10,9... | collective-permute-start | bytes 983048 | tf_op jit(solution)/shard_map/ppermute | solution.py:49
  18.6 0.7 copy-start.1
  21.4 8.2 %collective-permute-start.2 = (f32[5,16,8,32]{3,2,1,0:T(8,128)S(1)}, f32[5,16,8,32]{3,2,1,0:T(8,128)S(1)}, u32[]{:S(2)}, u32[]{:S(2)}) collective-permute-start(f32[5,16,8,32]{3,2,1,0:T(8,128)S(1)} %copy.4), channel_id=1, source_target_pairs={{0,224},{32,0},{64,32},{96,64},{128,96},{160,128},{192,160},{224,1... | collective-permute-start | bytes 245768 | tf_op jit(solution)/shard_map/ppermute | solution.py:60
  21.9 9.6 %copy-start = (f32[4,16,16,128]{3,2,1,0:T(8,128)S(1)}, f32[4,16,16,128]{3,2,1,0:T(8,128)}, u32[]{:S(2)}) copy-start(f32[4,16,16,128]{3,2,1,0:T(8,128)} %param.3) | copy-start | bytes 1572868
  21.9 8.1 %collective-permute-start.3 = (f32[5,16,8,32]{3,2,1,0:T(8,128)S(1)}, f32[5,16,8,32]{3,2,1,0:T(8,128)}, u32[]{:S(2)}, u32[]{:S(2)}) collective-permute-start(f32[5,16,8,32]{3,2,1,0:T(8,128)S(1)} %copy.6), channel_id=1, source_target_pairs={{0,32},{32,64},{64,96},{96,128},{128,160},{160,192},{192,224},{224... | collective-permute-start | bytes 245768 | tf_op jit(solution)/shard_map/ppermute | solution.py:59
  33.1 20.6 %copy-start.2 = (s32[128]{0:T(128)S(1)}, s32[128]{0:T(128)}, u32[]{:S(2)}) copy-start(s32[128]{0:T(128)} %param.5) | copy-start | bytes 1540
  42.8 24.2 %all-to-all-start = ((f32[32,2,16,128]{3,2,1,0:T(8,128)}), f32[32,2,16,128]{3,2,1,0:T(8,128)S(1)}, u32[]{:S(2)}, u32[]{:S(2)}) async-start(f32[32,2,16,128]{3,2,1,0:T(8,128)} %bitcast.6), calls=%async_computation | async-start | bytes 1048576 | tf_op jit(solution)/shard_map/all_to_all | solution.py:200
  92.3 8.6 %collective-permute-start.5 = (f32[4,16,8,32]{3,2,1,0:T(8,128)S(1)}, f32[4,16,8,32]{3,2,1,0:T(8,128)S(1)}, u32[]{:S(2)}, u32[]{:S(2)}) collective-permute-start(f32[4,16,8,32]{3,2,1,0:T(8,128)S(1)} %copy.10), channel_id=1, source_target_pairs={{0,32},{32,64},{64,96},{96,128},{128,160},{160,192},{192,224},{224... | collective-permute-start | bytes 196616 | tf_op jit(solution)/shard_map/ppermute | solution.py:59
  92.7 9.3 %collective-permute-start.4 = (f32[4,16,8,32]{3,2,1,0:T(8,128)S(1)}, f32[4,16,8,32]{3,2,1,0:T(8,128)}, u32[]{:S(2)}, u32[]{:S(2)}) collective-permute-start(f32[4,16,8,32]{3,2,1,0:T(8,128)S(1)} %copy.8), channel_id=1, source_target_pairs={{0,224},{32,0},{64,32},{96,64},{128,96},{160,128},{192,160},{224,1... | collective-permute-start | bytes 196616 | tf_op jit(solution)/shard_map/ppermute | solution.py:60

commit v5 on v4

--- a/solution.py
+++ b/solution.py
@@ -120,6 +120,7 @@
             values = state_ref[field, level]
             running_ref[field, level] = values[first:first + cells, :rows]
             even_ref[field, level] = jnp.where(keep, values, 0.0)
+        even_ref[4, level] = sound_ref[level] * even_ref[0, level]
         return carry
 
     lax.fori_loop(0, levels, start, 0)
@@ -138,7 +139,7 @@
 
             radial_flow = source[1, level]
             azimuth_flow = source[2, level]
-            pressure = sound_ref[level] * source[0, level]
+            pressure = source[4, level]
             density_rate = -(
                 lane_diff(radial_flow)[region]
                 + sublane_diff(azimuth_flow)[region]
@@ -148,13 +149,15 @@
             azimuth_rate = -sublane_diff(pressure)[region] - (
                 2.0 - SHEAR_RATE
             ) * ANGULAR_RATE * radial_flow[region]
-            vertical_rate = -vertical(lambda at: sound_ref[at][region] * source[0, at][region])
+            vertical_rate = -vertical(lambda at: source[4, at][region])
             rates = (density_rate, radial_rate, azimuth_rate, vertical_rate)
             inside = keep[:, region[1]]
             for field, rate in enumerate(rates):
                 series = jnp.where(inside, scale * rate, 0.0)
                 if not last:
                     target[field, level] = series
+                    if field == 0:
+                        target[4, level] = sound_ref[level] * series
                 own_part = series if last else series[first:first + cells, :rows]
                 running_ref[field, level] = running_ref[field, level] + own_part
             return carry
@@ -171,7 +174,7 @@
         out_shape=jax.ShapeDtypeStruct(wide_state.shape[:2] + (cells, row_count), jnp.float32),
         in_specs=[whole, whole, whole],
         out_specs=whole,
-        scratch_shapes=[pltpu.VMEM(wide_state.shape, jnp.float32)] * 2,
+        scratch_shapes=[pltpu.VMEM((5,) + wide_state.shape[1:], jnp.float32)] * 2,
         compiler_params=pltpu.CompilerParams(vmem_limit_bytes=48 * 1024 * 1024),
         cost_estimate=pl.CostEstimate(
             flops=60 * ORDER * size, transcendentals=0, bytes_accessed=4 * (2 * size + size // 4)

time: 152 us -> 152 us (level)
  no operation moved by 1% of the time
where the time goes in v5:
time: 152 us; the launch traced here: 150 us
  blocking collectives  53.3 us (35%)
  waiting for transfers between devices  37.3 us (25%)
  starting transfers between devices  21 us (14%)
  Pallas kernels  18.6 us (12%)
  local copies, waits for them, and re-layouts  11.6 us (8%)
  other arithmetic  7.28 us (5%)
    all_to_all x2, blocking collectives, remap(): planes = lax.all_to_all(blocks, 'azi', 0, 0, tiled=True)  36.9 us
    pallas_call x2, Pallas kernels, taylor(): pl.pallas_call(functools.partial(taylor_kernel, own=(depth, cells, row_co...  18.6 us
    all_to_all x1, blocking collectives, remap(): blocks = lax.all_to_all(planes, 'azi', 0, 0, tiled=True)  16.4 us
    all_to_all x1, waiting for transfers between devices, remap(): blocks = lax.all_to_all(planes, 'azi', 0, 0, tiled=True)  13.2 us
    all_to_all x1, starting transfers between devices, remap(): blocks = lax.all_to_all(planes, 'azi', 0, 0, tiled=True)  11 us
    ppermute x1, waiting for transfers between devices, azimuthal_halos(): lax.ppermute(cells[:, :, count - depth:, :], 'azi', ring('azi', 1))  8.39 us
    ppermute x2, waiting for transfers between devices, radial_halos(): high = jnp.swapaxes(lax.ppermute(high, 'rad', ring('rad', -1)), 2, 3)  7.89 us
    ppermute x2, waiting for transfers between devices, radial_halos(): low = jnp.swapaxes(lax.ppermute(low, 'rad', ring('rad', 1)), 2, 3)  5.54 us
  transfers between devices with their start and end apart: 7, of which 6 were waited for; matrix products, arithmetic and copies ran while one was open for 1% of the time, Pallas kernels for 0%

profile of v5, /device:TPU:64, one launch (start us, length us, event | category | flops | bytes accessed | tf_op | source)
XLA Modules:
  0.0 149.7 jit_solution(1648546327160984639)
XLA Ops:
  0.0 1.1 fusion.18
  1.1 2.0 %collective-permute-start = (f32[5,16,8,128]{3,2,1,0:T(8,128)S(1)}, f32[5,16,8,128]{3,2,1,0:T(8,128)S(1)}, u32[]{:S(2)}, u32[]{:S(2)}) collective-permute-start(f32[5,16,8,128]{3,2,1,0:T(8,128)S(1)} %get-tuple-element.9), channel_id=1, source_target_pairs={{0,1},{1,2},{2,3},{3,4},{4,5},{5,6},{6,7},{7,8},{8,9},{9,10},{10,1... | collective-permute-start | bytes 983048 | tf_op jit(solution)/shard_map/ppermute | solution.py:47
  3.1 4.7 %collective-permute-start.1 = (f32[5,16,8,128]{3,2,1,0:T(8,128)S(1)}, f32[5,16,8,128]{3,2,1,0:T(8,128)S(1)}, u32[]{:S(2)}, u32[]{:S(2)}) collective-permute-start(f32[5,16,8,128]{3,2,1,0:T(8,128)S(1)} %get-tuple-element.10), channel_id=1, source_target_pairs={{0,31},{1,0},{2,1},{3,2},{4,3},{5,4},{6,5},{7,6},{8,7},{9,8},{10,9... | collective-permute-start | bytes 983048 | tf_op jit(solution)/shard_map/ppermute | solution.py:49
  7.9 8.4 %collective-permute-done = f32[5,16,8,128]{3,2,1,0:T(8,128)S(1)} collective-permute-done((f32[5,16,8,128]{3,2,1,0:T(8,128)S(1)}, f32[5,16,8,128]{3,2,1,0:T(8,128)S(1)}, u32[]{:S(2)}, u32[]{:S(2)}) %collective-permute-start) | collective-permute-done | bytes 327712 | tf_op jit(solution)/shard_map/ppermute | solution.py:47
  16.3 2.3 %collective-permute-done.1 = f32[5,16,8,128]{3,2,1,0:T(8,128)S(1)} collective-permute-done((f32[5,16,8,128]{3,2,1,0:T(8,128)S(1)}, f32[5,16,8,128]{3,2,1,0:T(8,128)S(1)}, u32[]{:S(2)}, u32[]{:S(2)}) %collective-permute-start.1) | collective-permute-done | bytes 327712 | tf_op jit(solution)/shard_map/ppermute | solution.py:49
  18.6 0.7 copy-done.1
  19.3 1.2 pad_maximum_fusion.2
  20.5 0.5 slice_bitcast_fusion.1
  21.0 0.4 copy.4
  21.5 0.4 copy.6
  21.9 0.6 collective-permute-start.3
  22.4 7.1 %collective-permute-done.2 = f32[5,16,8,32]{3,2,1,0:T(8,128)S(1)} collective-permute-done((f32[5,16,8,32]{3,2,1,0:T(8,128)S(1)}, f32[5,16,8,32]{3,2,1,0:T(8,128)S(1)}, u32[]{:S(2)}, u32[]{:S(2)}) %collective-permute-start.2) | collective-permute-done | bytes 81952 | tf_op jit(solution)/shard_map/ppermute | solution.py:60
  29.6 0.4 copy.5
  30.0 1.4 copy.7
  31.4 1.5 %pad_maximum_fusion = f32[5,16,32,256]{3,2,1,0:T(8,128)S(1)} fusion(f32[5,16,32,8]{3,2,1,0:T(8,128)S(1)} %bitcast.35, f32[5,16,32,8]{3,2,1,0:T(8,128)S(1)} %bitcast.34, f32[5,16,8,128]{3,2,1,0:T(8,128)} %copy-done.1, f32[1,16,16,128]{3,2,1,0:T(8,128)} %bitcast.41, f32[4,16,16,128]{3,2,1,0:T(8,128)S(1)} %copy-done, ...), kind=kLoop, calls=%fused_computation | loop fusion | flops 3932160 | bytes 4097024 | tf_op jit(solution)/shard_map/concatenate | solution.py:63
  33.1 9.7 %shard_map.37 = f32[4,16,16,128]{3,2,1,0:T(8,128)} custom-call(f32[1,256]{1,0:T(1,128)S(1)} %and_convert_fusion.keep_ref, f32[16,32,256]{2,1,0:T(8,128)S(1)} %slice_bitcast_fusion.4.sound_ref, f32[4,16,32,256]{3,2,1,0:T(8,128)S(1)} %slice.281.state_ref), custom_call_target="tpu_custom_call" | custom-call | flops 125829120 | bytes 4718592 | tf_op jit(solution)/shard_map/pallas_call | solution.py:172
  42.8 11.0 %all-to-all-start = ((f32[32,2,16,128]{3,2,1,0:T(8,128)}), f32[32,2,16,128]{3,2,1,0:T(8,128)S(1)}, u32[]{:S(2)}, u32[]{:S(2)}) async-start(f32[32,2,16,128]{3,2,1,0:T(8,128)} %bitcast.6), calls=%async_computation | async-start | bytes 1048576 | tf_op jit(solution)/shard_map/all_to_all | solution.py:203
  53.8 13.2 %all-to-all-done = f32[32,2,16,128]{3,2,1,0:T(8,128)S(1)} async-done(((f32[32,2,16,128]{3,2,1,0:T(8,128)}), f32[32,2,16,128]{3,2,1,0:T(8,128)S(1)}, u32[]{:S(2)}, u32[]{:S(2)}) %all-to-all-start) | async-done | bytes 524320 | tf_op jit(solution)/shard_map/all_to_all | solution.py:203
  68.7 20.7 %all_to_all.20 = f32[32,2,32,128]{3,2,1,0:T(8,128)S(1)} all-to-all(f32[32,2,32,128]{3,2,1,0:T(8,128)S(1)} %fusion), channel_id=1, replica_groups=mesh['rad'=8,'azi'=32] {'azi'}, dimensions={0} | all-to-all | bytes 2097152 | tf_op jit(solution)/shard_map/all_to_all | solution.py:214
  89.4 1.4 slice_bitcast_fusion.3
  90.8 1.5 %copy.10 = f32[4,16,8,32]{3,2,1,0:T(8,128)S(1)} copy(f32[4,16,8,32]{2,3,1,0:T(8,128)} %get-tuple-element.8) | data formatting | bytes 131072 | tf_op jit(solution)/shard_map/transpose | solution.py:57
  92.4 0.3 copy.8
  92.7 2.7 %collective-permute-start.4 = (f32[4,16,8,32]{3,2,1,0:T(8,128)S(1)}, f32[4,16,8,32]{3,2,1,0:T(8,128)}, u32[]{:S(2)}, u32[]{:S(2)}) collective-permute-start(f32[4,16,8,32]{3,2,1,0:T(8,128)S(1)} %copy.8), channel_id=1, source_target_pairs={{0,224},{32,0},{64,32},{96,64},{128,96},{160,128},{192,160},{224,1... | collective-permute-start | bytes 196616 | tf_op jit(solution)/shard_map/ppermute | solution.py:60
  95.4 5.5 %collective-permute-done.5 = f32[4,16,8,32]{3,2,1,0:T(8,128)S(1)} collective-permute-done((f32[4,16,8,32]{3,2,1,0:T(8,128)S(1)}, f32[4,16,8,32]{3,2,1,0:T(8,128)S(1)}, u32[]{:S(2)}, u32[]{:S(2)}) %collective-permute-start.5) | collective-permute-done | bytes 65568 | tf_op jit(solution)/shard_map/ppermute | solution.py:59
  100.9 0.4 copy.11
  101.3 0.7 collective-permute-done.4
  102.1 2.3 %copy.9 = f32[4,16,8,32]{2,3,1,0:T(8,128)} copy(f32[4,16,8,32]{3,2,1,0:T(8,128)} %collective-permute-done.4) | data formatting | bytes 131072 | tf_op jit(solution)/shard_map/ppermute | solution.py:60
  104.4 1.6 %pad_maximum_fusion.1.state_ref = f32[4,16,32,256]{3,2,1,0:T(8,128)S(1)} fusion(f32[4,16,32,8]{3,2,1,0:T(8,128)S(1)} %bitcast.36, f32[4,16,32,8]{3,2,1,0:T(8,128)} %bitcast.37, f32[4,16,32,128]{3,2,1,0:T(8,128)S(1)} %bitcast.27, f32[256]{0:T(256)S(1)} %pad.68.clone), kind=kLoop, calls=%fused_computation.1 | loop fusion | flops 1572864 | bytes 3277824 | tf_op jit(solution)/shard_map/concatenate | solution.py:63
  106.0 8.9 %shard_map.38 = f32[4,16,16,128]{3,2,1,0:T(8,128)S(1)} custom-call(f32[1,256]{1,0:T(1,128)S(1)} %and_convert_fusion.keep_ref, f32[16,32,256]{2,1,0:T(8,128)S(1)} %slice_bitcast_fusion.4.sound_ref, f32[4,16,32,256]{3,2,1,0:T(8,128)S(1)} %pad_maximum_fusion.1.state_ref), custom_call_target="tpu_custom_call" | custom-call | flops 125829120 | bytes 4718592 | tf_op jit(solution)/shard_map/pallas_call | solution.py:172
  114.9 16.4 %all_to_all.21 = f32[32,2,16,128]{3,2,1,0:T(8,128)S(1)} all-to-all(f32[32,2,16,128]{3,2,1,0:T(8,128)S(1)} %bitcast.25), channel_id=1, replica_groups=mesh['rad'=8,'azi'=32] {'azi'}, dimensions={0} | all-to-all | bytes 1048576 | tf_op jit(solution)/shard_map/all_to_all | solution.py:203
  132.7 16.2 %all_to_all.22 = f32[32,2,16,128]{3,2,1,0:T(8,128)S(1)} all-to-all(f32[32,2,16,128]{3,2,1,0:T(8,128)S(1)} %maximum_select_fusion.9), channel_id=1, replica_groups=mesh['rad'=8,'azi'=32] {'azi'}, dimensions={0} | all-to-all | bytes 1048576 | tf_op jit(solution)/shard_map/all_to_all | solution.py:214
  148.9 0.8 copy.13
  (71 shorter events, 3.0 us)
Async XLA Ops:
  1.1 15.2 %collective-permute-start = (f32[5,16,8,128]{3,2,1,0:T(8,128)S(1)}, f32[5,16,8,128]{3,2,1,0:T(8,128)S(1)}, u32[]{:S(2)}, u32[]{:S(2)}) collective-permute-start(f32[5,16,8,128]{3,2,1,0:T(8,128)S(1)} %get-tuple-element.9), channel_id=1, source_target_pairs={{0,1},{1,2},{2,3},{3,4},{4,5},{5,6},{6,7},{7,8},{8,9},{9,10},{10,1... | collective-permute-start | bytes 983048 | tf_op jit(solution)/shard_map/ppermute | solution.py:47
  3.1 15.5 %collective-permute-start.1 = (f32[5,16,8,128]{3,2,1,0:T(8,128)S(1)}, f32[5,16,8,128]{3,2,1,0:T(8,128)S(1)}, u32[]{:S(2)}, u32[]{:S(2)}) collective-permute-start(f32[5,16,8,128]{3,2,1,0:T(8,128)S(1)} %get-tuple-element.10), channel_id=1, source_target_pairs={{0,31},{1,0},{2,1},{3,2},{4,3},{5,4},{6,5},{7,6},{8,7},{9,8},{10,9... | collective-permute-start | bytes 983048 | tf_op jit(solution)/shard_map/ppermute | solution.py:49
  18.6 0.7 copy-start.1
  21.4 8.2 %collective-permute-start.2 = (f32[5,16,8,32]{3,2,1,0:T(8,128)S(1)}, f32[5,16,8,32]{3,2,1,0:T(8,128)S(1)}, u32[]{:S(2)}, u32[]{:S(2)}) collective-permute-start(f32[5,16,8,32]{3,2,1,0:T(8,128)S(1)} %copy.4), channel_id=1, source_target_pairs={{0,224},{32,0},{64,32},{96,64},{128,96},{160,128},{192,160},{224,1... | collective-permute-start | bytes 245768 | tf_op jit(solution)/shard_map/ppermute | solution.py:60
  21.9 9.6 %copy-start = (f32[4,16,16,128]{3,2,1,0:T(8,128)S(1)}, f32[4,16,16,128]{3,2,1,0:T(8,128)}, u32[]{:S(2)}) copy-start(f32[4,16,16,128]{3,2,1,0:T(8,128)} %param.3) | copy-start | bytes 1572868
  21.9 8.1 %collective-permute-start.3 = (f32[5,16,8,32]{3,2,1,0:T(8,128)S(1)}, f32[5,16,8,32]{3,2,1,0:T(8,128)}, u32[]{:S(2)}, u32[]{:S(2)}) collective-permute-start(f32[5,16,8,32]{3,2,1,0:T(8,128)S(1)} %copy.6), channel_id=1, source_target_pairs={{0,32},{32,64},{64,96},{96,128},{128,160},{160,192},{192,224},{224... | collective-permute-start | bytes 245768 | tf_op jit(solution)/shard_map/ppermute | solution.py:59
  33.1 20.7 %copy-start.2 = (s32[128]{0:T(128)S(1)}, s32[128]{0:T(128)}, u32[]{:S(2)}) copy-start(s32[128]{0:T(128)} %param.5) | copy-start | bytes 1540
  42.8 24.2 %all-to-all-start = ((f32[32,2,16,128]{3,2,1,0:T(8,128)}), f32[32,2,16,128]{3,2,1,0:T(8,128)S(1)}, u32[]{:S(2)}, u32[]{:S(2)}) async-start(f32[32,2,16,128]{3,2,1,0:T(8,128)} %bitcast.6), calls=%async_computation | async-start | bytes 1048576 | tf_op jit(solution)/shard_map/all_to_all | solution.py:203
  92.3 8.6 %collective-permute-start.5 = (f32[4,16,8,32]{3,2,1,0:T(8,128)S(1)}, f32[4,16,8,32]{3,2,1,0:T(8,128)S(1)}, u32[]{:S(2)}, u32[]{:S(2)}) collective-permute-start(f32[4,16,8,32]{3,2,1,0:T(8,128)S(1)} %copy.10), channel_id=1, source_target_pairs={{0,32},{32,64},{64,96},{96,128},{128,160},{160,192},{192,224},{224... | collective-permute-start | bytes 196616 | tf_op jit(solution)/shard_map/ppermute | solution.py:59
  92.7 9.3 %collective-permute-start.4 = (f32[4,16,8,32]{3,2,1,0:T(8,128)S(1)}, f32[4,16,8,32]{3,2,1,0:T(8,128)}, u32[]{:S(2)}, u32[]{:S(2)}) collective-permute-start(f32[4,16,8,32]{3,2,1,0:T(8,128)S(1)} %copy.8), channel_id=1, source_target_pairs={{0,224},{32,0},{64,32},{96,64},{128,96},{160,128},{192,160},{224,1... | collective-permute-start | bytes 196616 | tf_op jit(solution)/shard_map/ppermute | solution.py:60
